TPU v7x, 128 devices: a whole 4x4x4 slice. The times are simulated.
128 devices in a mesh: dp: 32 (over y, x, core), tensor: 4 (over z).
Axes of the slice: x: 4, y: 4, z: 4, core: 2. Of those that a mesh axis runs over, the one named last changes fastest.
Arguments:
- layer_input: bfloat16 [4096, 2560], P('dp'), may hold values from -6 to 6
- inner_out: bfloat16 [4096, 2560], P('dp', 'tensor'), may hold values from -6 to 6
- out_grad: bfloat16 [4096, 2560], P('dp'), may hold values from -0.09375 to 0.09375
- zx_grad: bfloat16 [4096, 5120], P('dp', 'tensor'), may hold values from -0.09375 to 0.09375
- bc_grad: bfloat16 [4096, 1024], P('dp', 'tensor'), may hold values from -0.09375 to 0.09375
- dt_grad: bfloat16 [4096, 40], P('dp', 'tensor'), may hold values from -0.09375 to 0.09375
- owner_deal: int32 [4, 31], P('tensor'), may hold values from 0 to 31, as said below
- head_momentum: float32 [4, 2368, 2560], P('tensor', 'dp'), may hold values from -6 to 6
- bc_momentum: float32 [2, 128, 2560], replicated, may hold values from -6 to 6
Outputs:
- head_update: bfloat16 [40, 3, 64, 2560], P('tensor')
- dt_update: bfloat16 [40, 2560], P('tensor')
- bc_update: bfloat16 [2, 128, 2560], replicated
- head_momentum_out: float32 [4, 2368, 2560], P('tensor', 'dp')
- bc_momentum_out: float32 [2, 128, 2560], replicated
Inputs may be any that keep to these rules, and one draw needn't show every extreme that they name: `owner_deal`: each owner holds at most 1 head blocks of one tensor index; the owner of the dt block (the last entry) holds exactly 1 head blocks of that index as well, so it holds exactly 74 rows.
All inputs are finite; a program needn't handle non-finite values.
Results may differ from a plain program's by a relative error of at most 0.0085.
Values may be sent and summed in bfloat16 or wider, within the bound.
No kernel may reach another device: no remote copies, remote signals or barrier semaphores. Data moves between devices by JAX's collectives and lax.ppermute only.
A program may use at most 128 MiB of HBM per device.

v0:
```python
import math

import jax
import jax.numpy as jnp
import numpy as np
from jax import lax
from jax.sharding import PartitionSpec as P

HD = 64
STATE = 128
NS_ITERS = 5


quintic_first = 3.4445
quintic_second = -4.775
quintic_third = 2.0315
momentum_decay = 0.95
norm_epsilon = 1e-07


def orthogonalize(moment):
    highest = lax.Precision.HIGHEST
    norm_value = jnp.sqrt(jnp.sum(moment * moment, axis=(1, 2), keepdims=True))
    current = moment / (norm_value + norm_epsilon)
    for step in range(NS_ITERS):
        gram_matrix = jnp.einsum("bik,bjk->bij", current, current, precision=highest)
        polynomial = quintic_second * gram_matrix + quintic_third * jnp.einsum(
            "bij,bjk->bik", gram_matrix, gram_matrix, precision=highest
        )
        current = quintic_first * current + jnp.einsum(
            "bij,bjk->bik", polynomial, current, precision=highest
        )
    return current


def row_tables(heads_here, head_dim):
    block_of_row = np.concatenate(
        [np.repeat(np.arange(3 * heads_here), head_dim), np.full(heads_here, 3 * heads_here)]
    )
    within = np.concatenate([np.tile(np.arange(head_dim), 3 * heads_here), np.arange(heads_here)])
    return (block_of_row.astype(np.int32), within.astype(np.int32))


def slot_rows(owner_list, heads_here, head_dim, capacity):
    block_count = owner_list.shape[0]
    positions = jnp.arange(block_count, dtype=jnp.int32)
    block_sizes = jnp.where(positions < block_count - 1, head_dim, heads_here).astype(jnp.int32)
    same_owner = owner_list[:, None] == owner_list[None, :]
    earlier = positions[:, None] < positions[None, :]
    offsets = jnp.sum(jnp.where(same_owner & earlier, block_sizes[:, None], 0), axis=0)
    block_of_row, within = row_tables(heads_here, head_dim)
    block_ids = jnp.asarray(block_of_row)
    return (owner_list[block_ids] * capacity + offsets[block_ids] + jnp.asarray(within)).astype(
        jnp.int32
    )


def on_device(
    layer_input,
    inner_out,
    out_grad,
    zx_grad,
    bc_grad,
    dt_grad,
    owner_deal,
    head_momentum,
    bc_momentum,
):
    n_data = lax.axis_size("dp")
    heads_here = dt_grad.shape[1]
    width = layer_input.shape[1]
    capacity = head_momentum.shape[1]
    contract = (((0,), (0,)), ((), ()))
    zx_part = lax.dot_general(zx_grad, layer_input, contract, preferred_element_type=jnp.float32)
    out_part = lax.dot_general(inner_out, out_grad, contract, preferred_element_type=jnp.float32)
    dt_part = lax.dot_general(dt_grad, layer_input, contract, preferred_element_type=jnp.float32)
    head_rows = jnp.concatenate(
        [zx_part.reshape(heads_here, 2 * HD, width), out_part.reshape(heads_here, HD, width)],
        axis=1,
    ).reshape(3 * heads_here * HD, width)
    partial_rows = jnp.concatenate([head_rows, dt_part], axis=0).astype(jnp.bfloat16)
    rows_total = partial_rows.shape[0]
    slots = slot_rows(owner_deal[0], heads_here, HD, capacity)
    source = (
        jnp.full((n_data * capacity,), rows_total, jnp.int32)
        .at[slots]
        .set(jnp.arange(rows_total, dtype=jnp.int32))
    )
    padded_rows = jnp.concatenate([partial_rows, jnp.zeros((1, width), jnp.bfloat16)], axis=0)
    send_buffer = jnp.take(padded_rows, source, axis=0)
    received = lax.all_to_all(send_buffer, "dp", split_axis=0, concat_axis=0, tiled=True)
    owned_sum = jnp.sum(received.reshape(n_data, capacity, width), axis=0, dtype=jnp.float32)
    bc_part = lax.dot_general(bc_grad, layer_input, contract, preferred_element_type=jnp.float32)
    bc_rounded = lax.optimization_barrier(bc_part.astype(jnp.bfloat16)).astype(jnp.float32)
    bc_summed = lax.psum(bc_rounded, ("dp", "tensor"))
    moment = momentum_decay * head_momentum[0] + owned_sum
    slot_count = (capacity - heads_here) // HD + 1
    stacked = jnp.concatenate(
        [moment, jnp.zeros((slot_count * HD - capacity, width), jnp.float32)], axis=0
    ).reshape(slot_count, HD, width)
    direction = orthogonalize(stacked).reshape(slot_count * HD, width)[:capacity]
    owned_update = (direction * math.sqrt(width)).astype(jnp.bfloat16)
    everything = lax.all_gather(owned_update, "dp", axis=0, tiled=True)
    my_rows = jnp.take(everything, slots, axis=0)
    head_update = my_rows[: 3 * heads_here * HD].reshape(heads_here, 3, HD, width)
    dt_update = my_rows[3 * heads_here * HD :]
    bc_moment = momentum_decay * bc_momentum + bc_summed.reshape(2, STATE, width)
    bc_update = (orthogonalize(bc_moment) * math.sqrt(width)).astype(jnp.bfloat16)
    return (head_update, dt_update, bc_update, moment[None], bc_moment)


def solution(mesh):
    in_specs = (
        P("dp", None),
        P("dp", "tensor"),
        P("dp", None),
        P("dp", "tensor"),
        P("dp", "tensor"),
        P("dp", "tensor"),
        P("tensor", None),
        P("tensor", "dp", None),
        P(),
    )
    out_specs = (
        P("tensor", None, None, None),
        P("tensor", None),
        P(),
        P("tensor", "dp", None),
        P(),
    )
    return jax.shard_map(
        on_device, mesh=mesh, in_specs=in_specs, out_specs=out_specs, check_vma=False
    )
```

profile of v0, /device:TPU:1, one launch (start us, length us, event | category | flops | bytes accessed | tf_op | source)
XLA Modules:
  0.0 501.3 jit_solution(14550085660775130404)
XLA Ops:
  13.4 39.8 %compare_and_fusion.1 = (pred[1930]{0:T(1024)(128)(4,1)S(1)}, s32[1930]{0:T(1024)S(1)}) fusion(s32[1930]{0:T(1024)} %constant.41.clone, pred[1930]{0:T(1024)(128)(4,1)} %constant.146, pred[1930]{0:T(1024)(128)(4,1)} %constant.147, pred[1930]{0:T(1024)(128)(4,1)} %constant.148, pred[1930]{0:T(1024)(128)(4,1)} %constant.149, pred[1930]{0:T(1024)(128)(4,1)} %constant.150, ...), kind=kLoop, calls=%fused_computation.71 | loop fusion | flops 133170 | bytes 75518 | tf_op jit(solution)/shard_map/jit(_take)/and | solution.py:104
  53.1 10.0 %scatter_custom_fusion = s32[2368]{0:T(1024)S(1)} fusion(s32[1930]{0:T(1024)S(1)} %get-tuple-element.8, s32[1930]{0:T(1024)S(1)} %iota.15, s32[]{:T(128)} %constant.30.clone.1), kind=kCustom, calls=%fused_computation.72 | custom fusion | bytes 9476 | tf_op jit(solution)/shard_map/scatter | solution.py:87
  63.2 2.9 convolution_convert_fusion
  68.1 4.6 fusion.2
  72.7 28.9 %gather_fusion = bf16[2368,2560]{1,0:T(8,128)(2,1)} fusion(bf16[1931,2560]{1,0:T(8,128)(2,1)} %fusion.2, s32[3072]{0:T(1024)S(1)} %pad_clamp_fusion), kind=kCustom, calls=%fused_computation | custom fusion | bytes 24257792 | tf_op jit(solution)/shard_map/jit(_take)/gather | solution.py:90
  101.6 12.3 %gather.19 = bf16[32,74,2560]{2,1,0:T(8,128)(2,1)} reshape(bf16[2368,2560]{1,0:T(8,128)(2,1)} %gather_fusion) | data formatting | bytes 24248320 | tf_op jit(solution)/shard_map/jit(_take)/gather | solution.py:90
  114.1 6.7 %broadcast_select_fusion = bf16[32,74,2560]{2,1,0:T(8,128)(2,1)S(1)} fusion(bf16[32,74,2560]{2,1,0:T(8,128)(2,1)} %gather.19, pred[32,74]{1,0:T(8,128)(4,1)S(1)} %broadcast_in_dim.70), kind=kLoop, calls=%fused_computation.7 | loop fusion | flops 6062080 | bytes 24250688 | tf_op jit(solution)/shard_map/jit(_take)/select_n | solution.py:90
  120.8 154.7 %all_to_all.6 = bf16[32,74,2560]{2,1,0:T(8,128)(2,1)} all-to-all(bf16[32,74,2560]{2,1,0:T(8,128)(2,1)S(1)} %broadcast_select_fusion), channel_id=1, replica_groups=mesh['dp'=32,'tensor'=4] {'dp'}, dimensions={0} | all-to-all | bytes 24248320 | tf_op jit(solution)/shard_map/all_to_all | solution.py:91
  275.6 6.9 %convert_reduce_fusion = f32[74,2560]{1,0:T(8,128)S(1)} fusion(bf16[32,74,2560]{2,1,0:T(8,128)(2,1)} %all_to_all.6), kind=kLoop, calls=%fused_computation.3 | loop fusion | flops 11934720 | bytes 12881920 | tf_op jit(solution)/shard_map/reduce_sum | solution.py:92
  300.3 104.3 %all-reduce.3 = f32[2,128,2560]{2,1,0:T(8,128)S(1)} all-reduce(bf16[2,128,2560]{2,1,0:T(8,128)(2,1)} %bitcast.141), channel_id=1, replica_groups=mesh['dp'=32,'tensor'=4] {'dp','tensor'}, use_global_device_ids=true, to_apply=%region_5.6 | all-reduce | flops 655360 | bytes 3932160 | tf_op jit(solution)/shard_map/psum | solution.py:95
  406.9 2.8 fusion.16
  410.0 2.7 convolution_add_fusion.4
  412.7 2.5 fusion.31
  415.5 2.6 convolution_add_fusion.3
  418.1 2.9 fusion.32
  421.3 2.6 convolution_add_fusion.2
  424.0 2.5 fusion.33
  426.8 2.6 convolution_add_fusion.1
  429.4 2.5 fusion.34
  432.2 3.9 fusion.4
  438.1 12.4 %reshape.251 = bf16[2368,2560]{1,0:T(8,128)(2,1)} reshape(bf16[32,74,2560]{2,1,0:T(8,128)(2,1)} %all-gather.3.cloned.1.call-done) | data formatting | bytes 24248320
  450.5 25.3 %gather_fusion.1 = bf16[1930,2560]{1,0:T(8,128)(2,1)} fusion(bf16[2368,2560]{1,0:T(8,128)(2,1)} %reshape.251, s32[2048]{0:T(1024)S(1)} %pad_clamp_fusion.1), kind=kCustom, calls=%fused_computation.1 | custom fusion | bytes 19770920 | tf_op jit(solution)/shard_map/jit(_take)/gather | solution.py:104
  475.8 8.6 %broadcast_select_fusion.1 = bf16[1930,2560]{1,0:T(8,128)(2,1)} fusion(bf16[1930,2560]{1,0:T(8,128)(2,1)} %gather_fusion.1, pred[1930]{0:T(1024)(128)(4,1)S(1)} %get-tuple-element.7), kind=kLoop, calls=%fused_computation.10 | loop fusion | flops 4940800 | bytes 19765130 | tf_op jit(solution)/shard_map/jit(_take)/select_n | solution.py:104
  484.4 8.4 %slice.113 = bf16[1920,2560]{1,0:T(8,128)(2,1)} slice(bf16[1930,2560]{1,0:T(8,128)(2,1)} %broadcast_select_fusion.1), slice={[0:1920], [0:2560]} | slice | bytes 19660800 | tf_op jit(solution)/shard_map/slice | solution.py:105
  (72 shorter events, 33.1 us)
Async XLA Ops:
  7.2 56.0 %copy-start = (bf16[128,2560]{1,0:T(8,128)(2,1)S(1)}, bf16[128,2560]{1,0:T(8,128)(2,1)}, u32[]{:S(2)}) copy-start(bf16[128,2560]{1,0:T(8,128)(2,1)} %param.11) | copy-start | bytes 1966084
  7.2 430.9 %all-gather.3.cloned.1.call-start = ((), (), s32[]{:S(2)}) async-start(), calls=%async_computation.1 | async-start | bytes 13516800 | tf_op jit(solution)/shard_map/all_gather | solution.py:103
  63.1 3.0 copy-start.10
  63.2 3.2 copy-start.7
  63.2 3.2 copy-start.8
  275.6 6.9 %copy-start.4 = (f32[1,74,2560]{2,0,1:T(1,128)S(1)}, f32[1,74,2560]{2,0,1:T(1,128)}, u32[]{:S(2)}) copy-start(f32[1,74,2560]{2,0,1:T(1,128)} %param.18) | copy-start | bytes 2273284
  282.5 2.0 copy-start.2
  296.2 2.4 copy-start.9
  406.9 3.1 copy-start.6
  431.9 4.2 copy-start.5
  432.2 4.0 copy-start.3
  484.4 9.9 %copy-start.1 = (bf16[128,2560]{1,0:T(8,128)(2,1)S(1)}, bf16[128,2560]{1,0:T(8,128)(2,1)}, u32[]{:S(2)}) copy-start(bf16[128,2560]{1,0:T(8,128)(2,1)} %param.11) | copy-start | bytes 1966084
Sparse Core Ops, SparseCore 0:
  298.8 64.9 all-gather.2
where the time goes:
time: 511 us; the launch traced here: 501 us
  blocking collectives  259 us (51%)
  local copies, waits for them, and re-layouts  104 us (20%)
  other arithmetic  73.7 us (14%)
  matrix products  49.4 us (10%)
  between operations  14.7 us (3%)
    all_to_all x1, blocking collectives, on_device(): lax.all_to_all(send_buffer, 'dp', split_axis=0, concat_axis=0, tiled=True)  155 us
    psum x1, blocking collectives, on_device(): bc_summed = lax.psum(bc_rounded, ('dp', 'tensor'))  104 us
    gather x2, local copies, waits for them, and re-layouts, on_device(): send_buffer = jnp.take(padded_rows, source, axis=0)  41.3 us
    and x1, other arithmetic, on_device(): my_rows = jnp.take(everything, slots, axis=0)  39.8 us
    gather x1, local copies, waits for them, and re-layouts, on_device(): my_rows = jnp.take(everything, slots, axis=0)  25.3 us
    dot_general x10, matrix products, orthogonalize(): jnp.einsum('bij,bjk->bik', polynomial, current, precision=highest)  21.3 us
    dot_general x10, matrix products, orthogonalize(): jnp.einsum('bik,bjk->bij', current, current, precision=highest)  20.1 us
    unnamed x23, local copies, waits for them, and re-layouts  12.4 us
  transfers between devices with their start and end apart: 1, of which 0 were waited for; matrix products, arithmetic and copies ran while one was open for 7% of the time, Pallas kernels for 0%

commit v1 on v0

v1 whole, which is shorter than its diff:
```python
import math

import jax
import jax.numpy as jnp
from jax import lax
from jax.sharding import PartitionSpec as P

HD = 64
STATE = 128
NS_ITERS = 5

quintic_first = 3.4445
quintic_second = -4.775
quintic_third = 2.0315
momentum_decay = 0.95
norm_epsilon = 1e-07

HEAD_REDUCE = "all_to_all"


def orthogonalize(moment):
    highest = lax.Precision.HIGHEST
    norm_value = jnp.sqrt(jnp.sum(moment * moment, axis=(1, 2), keepdims=True))
    current = moment / (norm_value + norm_epsilon)
    for step in range(NS_ITERS):
        gram_matrix = jnp.einsum("bik,bjk->bij", current, current, precision=highest)
        polynomial = quintic_second * gram_matrix + quintic_third * jnp.einsum(
            "bij,bjk->bik", gram_matrix, gram_matrix, precision=highest
        )
        current = quintic_first * current + jnp.einsum(
            "bij,bjk->bik", polynomial, current, precision=highest
        )
    return current


def on_device(
    layer_input,
    inner_out,
    out_grad,
    zx_grad,
    bc_grad,
    dt_grad,
    owner_deal,
    head_momentum,
    bc_momentum,
):
    n_data = lax.axis_size("dp")
    tokens, width = layer_input.shape
    heads_here = dt_grad.shape[1]
    capacity = head_momentum.shape[1]
    n_blocks = 3 * heads_here
    contract = (((0,), (0,)), ((), ()))
    f32, bf16 = jnp.float32, jnp.bfloat16

    owners = owner_deal[0]
    head_owner = owners[:n_blocks]
    dt_owner = owners[n_blocks]
    slots = jnp.arange(n_data, dtype=jnp.int32)

    bc_cols = lax.psum(bc_grad.astype(f32), "tensor")
    bc_part = lax.dot_general(
        bc_cols,
        layer_input.astype(f32),
        contract,
        precision=lax.Precision.HIGHEST,
        preferred_element_type=f32,
    )
    bc_summed = lax.psum(bc_part, "dp")

    zx = zx_grad.reshape(tokens, heads_here, 2, HD)
    io = inner_out.reshape(tokens, heads_here, 1, HD)
    upper = jnp.concatenate([zx, jnp.zeros_like(io)], axis=2).reshape(tokens, n_blocks, HD)
    lower = jnp.concatenate([jnp.zeros_like(zx), io], axis=2).reshape(tokens, n_blocks, HD)
    grad_blocks = jnp.concatenate([upper, lower], axis=0)
    pick = (head_owner[None, :] == slots[:, None]).astype(bf16)
    owner_cols = jnp.einsum(
        "tbr,ob->tor", grad_blocks, pick, preferred_element_type=f32
    ).astype(bf16)
    dt_cols = jnp.concatenate([dt_grad, jnp.zeros_like(dt_grad)], axis=0)
    is_dt = (slots == dt_owner).astype(bf16)
    dt_owner_cols = dt_cols[:, None, :] * is_dt[None, :, None]
    send_cols = jnp.concatenate([owner_cols, dt_owner_cols], axis=2).reshape(
        2 * tokens, n_data * capacity
    )
    factors = jnp.concatenate([layer_input, out_grad], axis=0)
    send = lax.dot_general(send_cols, factors, contract, preferred_element_type=f32).astype(bf16)

    if HEAD_REDUCE == "all_to_all":
        received = lax.all_to_all(send, "dp", split_axis=0, concat_axis=0, tiled=True)
        owned_sum = jnp.sum(
            received.reshape(n_data, capacity, width).astype(f32), axis=0
        )
    else:
        owned_sum = lax.psum_scatter(send, "dp", scatter_dimension=0, tiled=True).astype(f32)

    moment = momentum_decay * head_momentum[0] + owned_sum
    head_direction = orthogonalize(moment[None, :HD])[0]
    dt_direction = orthogonalize(moment[None, HD:])[0]
    owned_update = (
        jnp.concatenate([head_direction, dt_direction], axis=0) * math.sqrt(width)
    ).astype(bf16)
    everything = lax.all_gather(owned_update, "dp", axis=0, tiled=False)
    head_update = jnp.take(everything[:, :HD], head_owner, axis=0, mode="clip").reshape(
        heads_here, 3, HD, width
    )
    dt_update = lax.dynamic_index_in_dim(everything, dt_owner, axis=0, keepdims=False)[HD:]

    bc_moment = momentum_decay * bc_momentum + bc_summed.reshape(2, STATE, width)
    bc_update = (orthogonalize(bc_moment) * math.sqrt(width)).astype(bf16)
    return (head_update, dt_update, bc_update, moment[None], bc_moment)


def solution(mesh):
    in_specs = (
        P("dp", None),
        P("dp", "tensor"),
        P("dp", None),
        P("dp", "tensor"),
        P("dp", "tensor"),
        P("dp", "tensor"),
        P("tensor", None),
        P("tensor", "dp", None),
        P(),
    )
    out_specs = (
        P("tensor", None, None, None),
        P("tensor", None),
        P(),
        P("tensor", "dp", None),
        P(),
    )
    return jax.shard_map(
        on_device, mesh=mesh, in_specs=in_specs, out_specs=out_specs, check_vma=False
    )
```

time: 511 us -> 381 us (0.75)
  blocking collectives: 259 us -> 17.5 us
  waiting for transfers between devices: 0.02 us -> 225 us
  local copies, waits for them, and re-layouts: 104 us -> 41 us
  other arithmetic: 73.7 us -> 13.3 us
  starting transfers between devices: 0.04 us -> 9.02 us
    all_to_all x1 -> x0, blocking collectives: 155 us -> none  [on_device(): lax.all_to_all(send_buffer, 'dp', split_axis=0, concat_axis=0, tiled=True)]
    all_to_all x0 -> x1, waiting for transfers between devices: none -> 140 us  [on_device(): lax.all_to_all(send, 'dp', split_axis=0, concat_axis=0, tiled=True)]
    psum x1, blocking collectives: 104 us -> 17.5 us  [on_device(): bc_cols = lax.psum(bc_grad.astype(f32), 'tensor')]
    gather x7 -> x1, local copies, waits for them, and re-layouts: 71.9 us -> 9.84 us  [on_device(): jnp.take(everything[:, :HD], head_owner, axis=0, mode='clip')]
    psum x0 -> x1, waiting for transfers between devices: none -> 53.1 us  [on_device(): bc_summed = lax.psum(bc_part, 'dp')]
    and x2 -> x0, other arithmetic: 39.8 us -> none  [the longest x1 39.8 us: on_device(): my_rows = jnp.take(everything, slots, axis=0)]
    all_gather x1, waiting for transfers between devices: 0.01 us -> 32.7 us  [on_device(): everything = lax.all_gather(owned_update, 'dp', axis=0, tiled=False)]
    select_n x4 -> x0, other arithmetic: 15.3 us -> none  [the longest x1 8.59 us: on_device(): my_rows = jnp.take(everything, slots, axis=0)]
  transfers between devices with their start and end apart: 1 -> 3, of which waited for: 0 -> 3; matrix products, arithmetic and copies ran while one was open for 7% -> 15% of each run, Pallas kernels for 0% -> 0%
where the time goes in v1:
time: 381 us; the launch traced here: 375 us
  waiting for transfers between devices  225 us (59%)
  matrix products  51 us (13%)
  local copies, waits for them, and re-layouts  41 us (11%)
  between operations  18 us (5%)
  blocking collectives  17.5 us (5%)
  other arithmetic  13.3 us (3%)
  starting transfers between devices  9.02 us (2%)
    all_to_all x1, waiting for transfers between devices, on_device(): lax.all_to_all(send, 'dp', split_axis=0, concat_axis=0, tiled=True)  140 us
    psum x1, waiting for transfers between devices, on_device(): bc_summed = lax.psum(bc_part, 'dp')  53.1 us
    all_gather x1, waiting for transfers between devices, on_device(): everything = lax.all_gather(owned_update, 'dp', axis=0, tiled=False)  32.7 us
    dot_general x15, matrix products, orthogonalize(): jnp.einsum('bij,bjk->bik', polynomial, current, precision=highest)  19.4 us
    dot_general x15, matrix products, orthogonalize(): jnp.einsum('bik,bjk->bij', current, current, precision=highest)  18.2 us
    psum x1, blocking collectives, on_device(): bc_cols = lax.psum(bc_grad.astype(f32), 'tensor')  17.5 us
    all_to_all x1, local copies, waits for them, and re-layouts, on_device(): lax.all_to_all(send, 'dp', split_axis=0, concat_axis=0, tiled=True)  12.3 us
    gather x1, local copies, waits for them, and re-layouts, on_device(): jnp.take(everything[:, :HD], head_owner, axis=0, mode='clip')  9.84 us
  transfers between devices with their start and end apart: 3, of which 3 were waited for; matrix products, arithmetic and copies ran while one was open for 15% of the time, Pallas kernels for 0%

profile of v1, /device:TPU:1, one launch (start us, length us, event | category | flops | bytes accessed | tf_op | source)
XLA Modules:
  0.0 375.2 jit_solution(5837344694989984997)
XLA Ops:
  15.2 7.2 %convolution_convert_fusion = bf16[2368,2560]{1,0:T(8,128)(2,1)} fusion(bf16[256,2368]{0,1:T(8,128)(2,1)S(1)} %reshape.316, bf16[128,2560]{1,0:T(8,128)(2,1)} %param.11, bf16[128,2560]{1,0:T(8,128)(2,1)S(1)} %copy-done.1), kind=kOutput, calls=%fused_computation.2 | convolution fusion | flops 3112468480 | bytes 14647296 | tf_op jit(solution)/shard_map/dot_general | solution.py:86
  22.4 12.3 %all_to_all.6 = bf16[32,74,2560]{2,1,0:T(8,128)(2,1)} reshape(bf16[2368,2560]{1,0:T(8,128)(2,1)} %convolution_convert_fusion) | data formatting | bytes 24248320 | tf_op jit(solution)/shard_map/all_to_all | solution.py:89
  34.7 8.8 %all-to-all-start = ((bf16[32,74,2560]{2,1,0:T(8,128)(2,1)}), bf16[32,74,2560]{2,1,0:T(8,128)(2,1)}, u32[]{:S(2)}, u32[]{:S(2)}) async-start(bf16[32,74,2560]{2,1,0:T(8,128)(2,1)} %all_to_all.6), calls=%async_computation | async-start | bytes 26214400 | tf_op jit(solution)/shard_map/all_to_all | solution.py:89
  43.6 17.5 %all-reduce.7 = f32[128,256]{1,0:T(8,128)S(1)} all-reduce(bf16[128,256]{1,0:T(8,128)(2,1)S(1)} %copy-done.3), channel_id=1, replica_groups=mesh['dp'=32,'tensor'=4] {'tensor'}, use_global_device_ids=true, to_apply=%region_3.0 | all-reduce | flops 32768 | bytes 196608 | tf_op jit(solution)/shard_map/psum | solution.py:60
  61.0 2.7 fusion.43
  64.0 139.6 %all-to-all-done = bf16[32,74,2560]{2,1,0:T(8,128)(2,1)} async-done(((bf16[32,74,2560]{2,1,0:T(8,128)(2,1)}), bf16[32,74,2560]{2,1,0:T(8,128)(2,1)}, u32[]{:S(2)}, u32[]{:S(2)}) %all-to-all-start) | async-done | bytes 12124192 | tf_op jit(solution)/shard_map/all_to_all | solution.py:89
  203.6 6.8 %convert_reduce_fusion = f32[74,2560]{1,0:T(8,128)S(1)} fusion(bf16[32,74,2560]{2,1,0:T(8,128)(2,1)} %all-to-all-done), kind=kLoop, calls=%fused_computation.1 | loop fusion | flops 11934720 | bytes 12881920 | tf_op jit(solution)/shard_map/reduce_sum | solution.py:90
  227.7 53.1 %all-reduce.6.cloned.1.call-done = f32[2,128,2560]{2,1,0:T(8,128)} async-done(((f32[2,128,2560]{2,1,0:T(8,128)}), f32[2,128,2560]{2,1,0:T(8,128)}) %all-reduce.6.cloned.1.call-update) | async-done | bytes 2621456 | tf_op jit(solution)/shard_map/psum | solution.py:68
  280.8 3.2 multiply_reduce_fusion
  284.0 3.0 fusion.27
  287.3 2.7 convolution_add_fusion.4
  289.9 2.5 fusion.44
  292.7 2.6 convolution_add_fusion.3
  295.4 2.9 fusion.45
  298.6 2.6 convolution_add_fusion.2
  301.2 2.5 fusion.46
  304.0 2.6 convolution_add_fusion.1
  306.7 2.5 fusion.47
  309.5 3.9 %fusion.1 = bf16[2,128,2560]{2,1,0:T(8,128)(2,1)} fusion(f32[2,128,128]{2,1,0:T(8,128)S(1)} %fusion.8, f32[2,128,2560]{2,1,0:T(8,128)S(1)} %convolution_add_fusion.1), kind=kOutput, calls=%fused_computation.9 | convolution fusion | flops 1009254400 | bytes 4063232 | tf_op jit(solution)/shard_map/bij,bjk->bik/dot_general | solution.py:30
  313.5 1.6 copy.33
  315.2 32.7 %all-gather.2.cloned.1.call-done = bf16[32,74,2560]{2,1,0:T(8,128)(2,1)} async-done(((bf16[1,74,2560]{2,1,0:T(8,128)(2,1)}), bf16[32,74,2560]{2,1,0:T(8,128)(2,1)}) %all-gather.2.cloned.1.call-update) | async-done | bytes 12124176 | tf_op jit(solution)/shard_map/all_gather | solution.py:102
  347.9 9.0 %slice.34 = bf16[32,64,2560]{2,1,0:T(8,128)(2,1)} slice(bf16[32,74,2560]{2,1,0:T(8,128)(2,1)} %all-gather.2.cloned.1.call-done), slice={[0:32], [0:64], [0:2560]} | slice | bytes 20971520 | tf_op jit(solution)/shard_map/slice | solution.py:103
  356.9 9.8 %gather_fusion = bf16[30,64,2560]{2,1,0:T(8,128)(2,1)} fusion(bf16[32,64,2560]{2,1,0:T(8,128)(2,1)} %slice.34, s32[1024]{0:T(1024)S(1)} %pad_clamp_fusion), kind=kCustom, calls=%fused_computation | custom fusion | bytes 19660920 | tf_op jit(solution)/shard_map/jit(_take)/gather | solution.py:103
  366.7 1.5 dynamic-slice_bitcast_fusion
  (69 shorter events, 23.5 us)
Async XLA Ops:
  14.1 1.1 copy-start.1
  34.7 8.8 %copy-start.3 = (bf16[128,256]{1,0:T(8,128)(2,1)S(1)}, bf16[128,256]{1,0:T(8,128)(2,1)}, u32[]{:S(2)}) copy-start(bf16[128,256]{1,0:T(8,128)(2,1)} %param.13) | copy-start | bytes 196612
  34.7 168.9 %all-to-all-start = ((bf16[32,74,2560]{2,1,0:T(8,128)(2,1)}), bf16[32,74,2560]{2,1,0:T(8,128)(2,1)}, u32[]{:S(2)}, u32[]{:S(2)}) async-start(bf16[32,74,2560]{2,1,0:T(8,128)(2,1)} %all_to_all.6), calls=%async_computation | async-start | bytes 26214400 | tf_op jit(solution)/shard_map/all_to_all | solution.py:89
  43.5 237.3 %all-reduce.6.cloned.1.call-start = ((), (), s32[]{:S(2)}) async-start(), calls=%async_computation.2 | async-start | bytes 5242880 | tf_op jit(solution)/shard_map/psum | solution.py:68
  63.8 146.7 %copy-start = (f32[1,74,2560]{2,0,1:T(1,128)S(1)}, f32[1,74,2560]{2,0,1:T(1,128)}, u32[]{:S(2)}) copy-start(f32[1,74,2560]{2,0,1:T(1,128)} %param.16) | copy-start | bytes 2273284
  63.8 284.1 %all-gather.2.cloned.1.call-start = ((), (), s32[]{:S(2)}) async-start(), calls=%async_computation.1 | async-start | bytes 13516800 | tf_op jit(solution)/shard_map/all_gather | solution.py:102
  284.0 3.3 copy-start.2
Sparse Core Ops, SparseCore 0:
  63.9 216.9 all-reduce.5
  283.7 64.1 all-gather.1

commit v2 on v1

--- a/solution.py
+++ b/solution.py
@@ -14,9 +14,6 @@
 quintic_third = 2.0315
 momentum_decay = 0.95
 norm_epsilon = 1e-07
-
-HEAD_REDUCE = "all_to_all"
-
 
 def orthogonalize(moment):
     highest = lax.Precision.HIGHEST
@@ -57,7 +54,7 @@
     dt_owner = owners[n_blocks]
     slots = jnp.arange(n_data, dtype=jnp.int32)
 
-    bc_cols = lax.psum(bc_grad.astype(f32), "tensor")
+    bc_cols = jnp.sum(lax.all_gather(bc_grad, "tensor", axis=0).astype(f32), axis=0)
     bc_part = lax.dot_general(
         bc_cols,
         layer_input.astype(f32),
@@ -79,31 +76,27 @@
     dt_cols = jnp.concatenate([dt_grad, jnp.zeros_like(dt_grad)], axis=0)
     is_dt = (slots == dt_owner).astype(bf16)
     dt_owner_cols = dt_cols[:, None, :] * is_dt[None, :, None]
-    send_cols = jnp.concatenate([owner_cols, dt_owner_cols], axis=2).reshape(
-        2 * tokens, n_data * capacity
+    chunk = -(-capacity // 16) * 16
+    pad_cols = jnp.zeros((2 * tokens, n_data, chunk - capacity), bf16)
+    send_cols = jnp.concatenate([owner_cols, dt_owner_cols, pad_cols], axis=2).reshape(
+        2 * tokens, n_data * chunk
     )
     factors = jnp.concatenate([layer_input, out_grad], axis=0)
     send = lax.dot_general(send_cols, factors, contract, preferred_element_type=f32).astype(bf16)
-
-    if HEAD_REDUCE == "all_to_all":
-        received = lax.all_to_all(send, "dp", split_axis=0, concat_axis=0, tiled=True)
-        owned_sum = jnp.sum(
-            received.reshape(n_data, capacity, width).astype(f32), axis=0
-        )
-    else:
-        owned_sum = lax.psum_scatter(send, "dp", scatter_dimension=0, tiled=True).astype(f32)
+    owned_sum = lax.psum_scatter(send, "dp", scatter_dimension=0, tiled=True)[:capacity].astype(f32)
 
     moment = momentum_decay * head_momentum[0] + owned_sum
     head_direction = orthogonalize(moment[None, :HD])[0]
     dt_direction = orthogonalize(moment[None, HD:])[0]
-    owned_update = (
-        jnp.concatenate([head_direction, dt_direction], axis=0) * math.sqrt(width)
-    ).astype(bf16)
-    everything = lax.all_gather(owned_update, "dp", axis=0, tiled=False)
-    head_update = jnp.take(everything[:, :HD], head_owner, axis=0, mode="clip").reshape(
+    head_gathered = lax.all_gather(
+        (head_direction * math.sqrt(width)).astype(bf16), "dp", axis=0, tiled=False
+    )
+    tail = jnp.concatenate([dt_direction, jnp.zeros((chunk - capacity, width), f32)], axis=0)
+    tail_gathered = lax.all_gather((tail * math.sqrt(width)).astype(bf16), "dp", axis=0, tiled=False)
+    head_update = jnp.take(head_gathered, head_owner, axis=0, mode="clip").reshape(
         heads_here, 3, HD, width
     )
-    dt_update = lax.dynamic_index_in_dim(everything, dt_owner, axis=0, keepdims=False)[HD:]
+    dt_update = lax.dynamic_slice(tail_gathered, (dt_owner, 0, 0), (1, heads_here, width))[0]
 
     bc_moment = momentum_decay * bc_momentum + bc_summed.reshape(2, STATE, width)
     bc_update = (orthogonalize(bc_moment) * math.sqrt(width)).astype(bf16)

time: 381 us -> 372 us (0.976)
  waiting for transfers between devices: 225 us -> 258 us
  local copies, waits for them, and re-layouts: 41 us -> 20.6 us
  starting transfers between devices: 9.02 us -> 0.34 us
  other arithmetic: 13.3 us -> 6.46 us
  blocking collectives: 17.5 us -> 12.3 us
    all_to_all x1 -> x0, waiting for transfers between devices: 140 us -> none  [on_device(): lax.all_to_all(send, 'dp', split_axis=0, concat_axis=0, tiled=True)]
    reduce_scatter x0 -> x1, waiting for transfers between devices: none -> 91.4 us  [on_device(): lax.psum_scatter(send, 'dp', scatter_dimension=0, tiled=True)[:capacity]]
    psum x1, waiting for transfers between devices: 53.1 us -> 93.8 us  [on_device(): bc_summed = lax.psum(bc_part, 'dp')]
    all_gather x1 -> x2, waiting for transfers between devices: 32.7 us -> 72.5 us  [the longest x1 58.2 us: on_device(): lax.all_gather((head_direction * math.sqrt(width)).astype(bf16), 'dp', ax...]
    psum x1 -> x0, blocking collectives: 17.5 us -> none  [on_device(): bc_cols = lax.psum(bc_grad.astype(f32), 'tensor')]
    all_to_all x1 -> x0, local copies, waits for them, and re-layouts: 12.3 us -> none  [on_device(): lax.all_to_all(send, 'dp', split_axis=0, concat_axis=0, tiled=True)]
    all_gather x0 -> x1, blocking collectives: none -> 12.3 us  [on_device(): lax.all_gather(bc_grad, 'tensor', axis=0).astype(f32)]
    slice x2 -> x0, local copies, waits for them, and re-layouts: 10.5 us -> none  [the longest x1 8.96 us: on_device(): everything[:, :HD]]
  transfers between devices with their start and end apart: 3 -> 4, of which waited for: 3 -> 4; matrix products, arithmetic and copies ran while one was open for 15% -> 14% of each run, Pallas kernels for 0% -> 0%
where the time goes in v2:
time: 372 us; the launch traced here: 366 us
  waiting for transfers between devices  258 us (69%)
  matrix products  50.9 us (14%)
  local copies, waits for them, and re-layouts  20.6 us (6%)
  between operations  17.9 us (5%)
  blocking collectives  12.3 us (3%)
  other arithmetic  6.46 us (2%)
    psum x1, waiting for transfers between devices, on_device(): bc_summed = lax.psum(bc_part, 'dp')  93.8 us
    reduce_scatter x1, waiting for transfers between devices, on_device(): lax.psum_scatter(send, 'dp', scatter_dimension=0, tiled=True)[:capacity]  91.4 us
    all_gather x1, waiting for transfers between devices, on_device(): lax.all_gather((head_direction * math.sqrt(width)).astype(bf16), 'dp', ax...  58.2 us
    dot_general x15, matrix products, orthogonalize(): jnp.einsum('bij,bjk->bik', polynomial, current, precision=highest)  20.2 us
    dot_general x15, matrix products, orthogonalize(): jnp.einsum('bik,bjk->bij', current, current, precision=highest)  17.8 us
    all_gather x1, waiting for transfers between devices, on_device(): lax.all_gather((tail * math.sqrt(width)).astype(bf16), 'dp', axis=0, tile...  14.3 us
    all_gather x1, blocking collectives, on_device(): lax.all_gather(bc_grad, 'tensor', axis=0).astype(f32)  12.3 us
    gather x1, local copies, waits for them, and re-layouts, on_device(): jnp.take(head_gathered, head_owner, axis=0, mode='clip')  9.86 us
  transfers between devices with their start and end apart: 4, of which 4 were waited for; matrix products, arithmetic and copies ran while one was open for 14% of the time, Pallas kernels for 0%

profile of v2, /device:TPU:1, one launch (start us, length us, event | category | flops | bytes accessed | tf_op | source)
XLA Modules:
  0.0 366.4 jit_solution(17709010283561353093)
XLA Ops:
  7.2 1.2 slice.18
  12.0 1.2 copy.19
  15.4 6.7 %convolution_convert_fusion = bf16[2560,2560]{1,0:T(8,128)(2,1)} fusion(bf16[256,2560]{0,1:T(8,128)(2,1)S(1)} %bitcast.114, bf16[128,2560]{1,0:T(8,128)(2,1)S(1)} %copy-done.4, bf16[128,2560]{1,0:T(8,128)(2,1)S(1)} %copy-done), kind=kOutput, calls=%fused_computation.1 | convolution fusion | flops 3364618240 | bytes 15728640 | tf_op jit(solution)/shard_map/dot_general | solution.py:85
  23.0 12.3 %all-gather.2 = bf16[512,256]{1,0:T(8,128)(2,1)S(1)} all-gather(bf16[128,256]{1,0:T(8,128)(2,1)S(1)} %copy-done.5), channel_id=4, replica_groups=mesh['dp'=32,'tensor'=4] {'tensor'}, dimensions={0}, use_global_device_ids=true | all-gather | bytes 327680 | tf_op jit(solution)/shard_map/all_gather | solution.py:57
  35.3 2.7 fusion.42
  38.1 91.4 %reduce-scatter.2.cloned.1.call-done = bf16[80,2560]{1,0:T(8,128)(2,1)} async-done(((bf16[2560,2560]{1,0:T(8,128)(2,1)}), bf16[80,2560]{1,0:T(8,128)(2,1)}) %reduce-scatter.2.cloned.1.call-update) | async-done | bytes 409616 | tf_op jit(solution)/shard_map/reduce_scatter | solution.py:86
  145.3 1.4 fusion.3
  148.7 93.8 %all-reduce.6.cloned.1.call-done = f32[2,128,2560]{2,1,0:T(8,128)} async-done(((f32[2,128,2560]{2,1,0:T(8,128)}), f32[2,128,2560]{2,1,0:T(8,128)}) %all-reduce.6.cloned.1.call-update) | async-done | bytes 2621456 | tf_op jit(solution)/shard_map/psum | solution.py:65
  242.5 2.3 multiply_reduce_fusion
  244.8 2.8 fusion.26
  247.9 2.9 convolution_add_fusion.4
  250.8 2.5 fusion.43
  253.6 2.6 convolution_add_fusion.3
  256.2 2.5 fusion.44
  259.0 2.6 convolution_add_fusion.2
  261.7 2.8 fusion.45
  264.7 2.6 convolution_add_fusion.1
  267.4 2.5 fusion.46
  270.2 3.7 %fusion.1 = bf16[2,128,2560]{2,1,0:T(8,128)(2,1)} fusion(f32[2,128,128]{2,1,0:T(8,128)S(1)} %fusion.8, f32[2,128,2560]{2,1,0:T(8,128)S(1)} %convolution_add_fusion.1), kind=kOutput, calls=%fused_computation.8 | convolution fusion | flops 1009254400 | bytes 4063232 | tf_op jit(solution)/shard_map/bij,bjk->bik/dot_general | solution.py:27
  273.9 1.6 copy.25
  275.5 14.3 %all-gather.8.cloned.1.call-done = bf16[512,2560]{1,0:T(8,128)(2,1)} async-done(((bf16[16,2560]{1,0:T(8,128)(2,1)}), bf16[512,2560]{1,0:T(8,128)(2,1)}) %all-gather.8.cloned.1.call-update) | async-done | bytes 2621456 | tf_op jit(solution)/shard_map/all_gather | solution.py:95
  289.8 1.5 dynamic-slice_bitcast_fusion
  291.4 58.2 %all-gather.6.cloned.1.call-done = bf16[2048,2560]{1,0:T(8,128)(2,1)} async-done(((bf16[64,2560]{1,0:T(8,128)(2,1)}), bf16[2048,2560]{1,0:T(8,128)(2,1)}) %all-gather.6.cloned.1.call-update) | async-done | bytes 10485776 | tf_op jit(solution)/shard_map/all_gather | solution.py:91
  349.5 9.9 %gather_fusion = bf16[30,64,2560]{2,1,0:T(8,128)(2,1)} fusion(bf16[32,64,2560]{2,1,0:T(8,128)(2,1)} %bitcast.112, s32[1024]{0:T(1024)S(1)} %pad_clamp_fusion), kind=kCustom, calls=%fused_computation | custom fusion | bytes 19660920 | tf_op jit(solution)/shard_map/jit(_take)/gather | solution.py:96
  (75 shorter events, 22.2 us)
Async XLA Ops:
  7.2 122.4 %reduce-scatter.2.cloned.1.call-start = ((), (), s32[]{:S(2)}) async-start(), calls=%async_computation.1 | async-start | bytes 13516800 | tf_op jit(solution)/shard_map/reduce_scatter | solution.py:86
  14.1 1.1 copy-start
  14.2 1.3 copy-start.4
  22.1 0.8 copy-start.5
  22.2 220.3 %all-reduce.6.cloned.1.call-start = ((), (), s32[]{:S(2)}) async-start(), calls=%async_computation.2 | async-start | bytes 5242880 | tf_op jit(solution)/shard_map/psum | solution.py:65
  35.3 94.3 %copy-start.3 = (f32[1,74,2560]{2,0,1:T(1,128)S(1)}, f32[1,74,2560]{2,0,1:T(1,128)}, u32[]{:S(2)}) copy-start(f32[1,74,2560]{2,0,1:T(1,128)} %param.16) | copy-start | bytes 2273284
  38.1 251.8 %all-gather.8.cloned.1.call-start = ((), (), s32[]{:S(2)}) async-start(), calls=%async_computation.4 | async-start | bytes 2703360 | tf_op jit(solution)/shard_map/all_gather | solution.py:95
  136.6 213.0 %all-gather.6.cloned.1.call-start = ((), (), s32[]{:S(2)}) async-start(), calls=%async_computation.3 | async-start | bytes 10813440 | tf_op jit(solution)/shard_map/all_gather | solution.py:91
  142.9 99.6 %copy-start.1 = (f32[2,128,2560]{2,1,0:T(8,128)S(1)}, f32[2,128,2560]{2,1,0:T(8,128)}, u32[]{:S(2)}) copy-start(f32[2,128,2560]{2,1,0:T(8,128)} %param.17) | copy-start | bytes 7864324
  244.8 3.1 copy-start.2
Sparse Core Ops, SparseCore 0:
  22.3 107.2 reduce-scatter.1
  133.4 109.0 all-reduce.5
  245.3 44.4 all-gather.7
  292.5 56.9 all-gather.5

commit v3 on v2

--- a/solution.py
+++ b/solution.py
@@ -3,6 +3,8 @@
 import jax
 import jax.numpy as jnp
 from jax import lax
+from jax.experimental import pallas as pl
+from jax.experimental.pallas import tpu as pltpu
 from jax.sharding import PartitionSpec as P
 
 HD = 64
@@ -16,7 +18,7 @@
 norm_epsilon = 1e-07
 
 def orthogonalize(moment):
-    highest = lax.Precision.HIGHEST
+    highest = lax.Precision.HIGH
     norm_value = jnp.sqrt(jnp.sum(moment * moment, axis=(1, 2), keepdims=True))
     current = moment / (norm_value + norm_epsilon)
     for step in range(NS_ITERS):
@@ -28,6 +30,39 @@
             "bij,bjk->bik", polynomial, current, precision=highest
         )
     return current
+
+
+def _gather_kernel(index_ref, source_ref, out_ref, sems):
+    rows = out_ref.shape[1]
+    copies = []
+    for b in range(out_ref.shape[0]):
+        copy = pltpu.make_async_copy(
+            source_ref.at[index_ref[b], pl.ds(0, rows)], out_ref.at[b], sems.at[b]
+        )
+        copy.start()
+        copies.append(copy)
+    for copy in copies:
+        copy.wait()
+
+
+def gather_slabs(source, index, rows):
+    count = index.shape[0]
+    n, chunk, width = source.shape
+    index = jnp.clip(index, 0, n - 1).astype(jnp.int32)
+    return pl.pallas_call(
+        _gather_kernel,
+        grid_spec=pltpu.PrefetchScalarGridSpec(
+            num_scalar_prefetch=1,
+            grid=(),
+            in_specs=[pl.BlockSpec(memory_space=pl.ANY)],
+            out_specs=pl.BlockSpec(memory_space=pltpu.VMEM),
+            scratch_shapes=[pltpu.SemaphoreType.DMA((count,))],
+        ),
+        out_shape=jax.ShapeDtypeStruct((count, rows, width), source.dtype),
+        cost_estimate=pl.CostEstimate(
+            flops=0, transcendentals=0, bytes_accessed=2 * count * rows * width * source.dtype.itemsize
+        ),
+    )(index, source)
 
 
 def on_device(
@@ -55,14 +90,27 @@
     slots = jnp.arange(n_data, dtype=jnp.int32)
 
     bc_cols = jnp.sum(lax.all_gather(bc_grad, "tensor", axis=0).astype(f32), axis=0)
+    bc_total = bc_cols.shape[1]
+    bc_rows = bc_total // n_data
     bc_part = lax.dot_general(
         bc_cols,
         layer_input.astype(f32),
         contract,
         precision=lax.Precision.HIGHEST,
         preferred_element_type=f32,
-    )
-    bc_summed = lax.psum(bc_part, "dp")
+    ).astype(bf16)
+    bc_pieces = lax.all_to_all(bc_part, "dp", split_axis=0, concat_axis=0, tiled=True)
+    bc_sum_rows = jnp.sum(bc_pieces.reshape(n_data, bc_rows, width).astype(f32), axis=0)
+    me = lax.axis_index("dp")
+    bc_flat = bc_momentum.reshape(bc_total, width)
+    bc_moment_rows = momentum_decay * lax.dynamic_slice_in_dim(
+        bc_flat, me * bc_rows, bc_rows, axis=0
+    ) + bc_sum_rows
+    bc_copies = jnp.broadcast_to(bc_moment_rows[None], (n_data, bc_rows, width))
+    bc_moment = lax.all_to_all(bc_copies, "dp", split_axis=0, concat_axis=0, tiled=True)
+    bc_moment = bc_moment.reshape(2, STATE, width)
+    scale = math.sqrt(width)
+    bc_update = (orthogonalize(bc_moment) * scale).astype(bf16)
 
     zx = zx_grad.reshape(tokens, heads_here, 2, HD)
     io = inner_out.reshape(tokens, heads_here, 1, HD)
@@ -83,23 +131,23 @@
     )
     factors = jnp.concatenate([layer_input, out_grad], axis=0)
     send = lax.dot_general(send_cols, factors, contract, preferred_element_type=f32).astype(bf16)
-    owned_sum = lax.psum_scatter(send, "dp", scatter_dimension=0, tiled=True)[:capacity].astype(f32)
+    owned = lax.psum_scatter(send, "dp", scatter_dimension=0, tiled=True).astype(f32)
+    owned_sum = owned[:capacity]
 
     moment = momentum_decay * head_momentum[0] + owned_sum
     head_direction = orthogonalize(moment[None, :HD])[0]
     dt_direction = orthogonalize(moment[None, HD:])[0]
-    head_gathered = lax.all_gather(
-        (head_direction * math.sqrt(width)).astype(bf16), "dp", axis=0, tiled=False
+    owned_update = jnp.concatenate(
+        [
+            (head_direction * scale).astype(bf16),
+            (dt_direction * scale).astype(bf16),
+            jnp.zeros((chunk - capacity, width), bf16),
+        ],
+        axis=0,
     )
-    tail = jnp.concatenate([dt_direction, jnp.zeros((chunk - capacity, width), f32)], axis=0)
-    tail_gathered = lax.all_gather((tail * math.sqrt(width)).astype(bf16), "dp", axis=0, tiled=False)
-    head_update = jnp.take(head_gathered, head_owner, axis=0, mode="clip").reshape(
-        heads_here, 3, HD, width
-    )
-    dt_update = lax.dynamic_slice(tail_gathered, (dt_owner, 0, 0), (1, heads_here, width))[0]
-
-    bc_moment = momentum_decay * bc_momentum + bc_summed.reshape(2, STATE, width)
-    bc_update = (orthogonalize(bc_moment) * math.sqrt(width)).astype(bf16)
+    everything = lax.all_gather(owned_update, "dp", axis=0, tiled=False)
+    head_update = gather_slabs(everything, head_owner, HD).reshape(heads_here, 3, HD, width)
+    dt_update = lax.dynamic_slice(everything, (dt_owner, HD, 0), (1, heads_here, width))[0]
     return (head_update, dt_update, bc_update, moment[None], bc_moment)
 
 

time: 372 us -> 282 us (0.76)
  waiting for transfers between devices: 258 us -> 173 us
  matrix products: 50.9 us -> 34.6 us
  starting transfers between devices: 0.34 us -> 15.7 us
  Pallas kernels: 0 us -> 8.58 us
  local copies, waits for them, and re-layouts: 20.6 us -> 13.4 us
    psum x1 -> x0, waiting for transfers between devices: 93.8 us -> none  [on_device(): bc_summed = lax.psum(bc_part, 'dp')]
    all_gather x2 -> x1, waiting for transfers between devices: 72.5 us -> 0.01 us  [on_device(): everything = lax.all_gather(owned_update, 'dp', axis=0, tiled=False)]
    all_to_all x0 -> x2, waiting for transfers between devices: none -> 65.8 us  [the longest x1 46.6 us: on_device(): lax.all_to_all(bc_copies, 'dp', split_axis=0, concat_axis=0, tiled=True)]
    reduce_scatter x1, waiting for transfers between devices: 91.4 us -> 107 us  [on_device(): lax.psum_scatter(send, 'dp', scatter_dimension=0, tiled=True).astype(f32)]
    all_to_all x0 -> x2, starting transfers between devices: none -> 15.6 us  [the longest x1 10.1 us: on_device(): lax.all_to_all(bc_part, 'dp', split_axis=0, concat_axis=0, tiled=True)]
    gather x1 -> x0, local copies, waits for them, and re-layouts: 9.86 us -> none  [on_device(): jnp.take(head_gathered, head_owner, axis=0, mode='clip')]
    pallas_call x0 -> x1, Pallas kernels: none -> 8.58 us  [gather_slabs(): pl.pallas_call(_gather_kernel, grid_spec=pltpu.PrefetchScalarGridSpec(num...]
    dot_general x15, matrix products: 20.2 us -> 12.3 us  [orthogonalize(): jnp.einsum('bij,bjk->bik', polynomial, current, precision=highest)]
  transfers between devices with their start and end apart: 4 -> 4, of which waited for: 4 -> 3; matrix products, arithmetic and copies ran while one was open for 14% -> 9% of each run, Pallas kernels for 0% -> 0%
where the time goes in v3:
time: 282 us; the launch traced here: 279 us
  waiting for transfers between devices  173 us (61%)
  matrix products  34.6 us (12%)
  between operations  17.7 us (6%)
  starting transfers between devices  15.7 us (6%)
  local copies, waits for them, and re-layouts  13.4 us (5%)
  blocking collectives  9.8 us (3%)
  Pallas kernels  8.58 us (3%)
  other arithmetic  6.47 us (2%)
    reduce_scatter x1, waiting for transfers between devices, on_device(): lax.psum_scatter(send, 'dp', scatter_dimension=0, tiled=True).astype(f32)  107 us
    all_to_all x1, waiting for transfers between devices, on_device(): lax.all_to_all(bc_copies, 'dp', split_axis=0, concat_axis=0, tiled=True)  46.6 us
    all_to_all x1, waiting for transfers between devices, on_device(): lax.all_to_all(bc_part, 'dp', split_axis=0, concat_axis=0, tiled=True)  19.3 us
    dot_general x15, matrix products, orthogonalize(): jnp.einsum('bij,bjk->bik', polynomial, current, precision=highest)  12.3 us
    dot_general x15, matrix products, orthogonalize(): jnp.einsum('bik,bjk->bij', current, current, precision=highest)  10.4 us
    all_to_all x1, starting transfers between devices, on_device(): lax.all_to_all(bc_part, 'dp', split_axis=0, concat_axis=0, tiled=True)  10.1 us
    all_gather x1, blocking collectives, on_device(): lax.all_gather(bc_grad, 'tensor', axis=0).astype(f32)  9.8 us
    pallas_call x1, Pallas kernels, gather_slabs(): pl.pallas_call(_gather_kernel, grid_spec=pltpu.PrefetchScalarGridSpec(num...  8.58 us
  transfers between devices with their start and end apart: 4, of which 3 were waited for; matrix products, arithmetic and copies ran while one was open for 9% of the time, Pallas kernels for 0%

profile of v3, /device:TPU:1, one launch (start us, length us, event | category | flops | bytes accessed | tf_op | source)
XLA Modules:
  0.0 279.5 jit_solution(6285969163364166960)
XLA Ops:
  7.2 1.2 slice.24
  15.4 6.6 %convolution_convert_fusion = bf16[2560,2560]{1,0:T(8,128)(2,1)} fusion(bf16[256,2560]{0,1:T(8,128)(2,1)S(1)} %bitcast.121, bf16[128,2560]{1,0:T(8,128)(2,1)S(1)} %copy-done.2, bf16[128,2560]{1,0:T(8,128)(2,1)S(1)} %copy-done), kind=kOutput, calls=%fused_computation | convolution fusion | flops 3364618240 | bytes 15728640 | tf_op jit(solution)/shard_map/dot_general | solution.py:133
  22.1 107.4 %reduce-scatter.2.cloned.1.call-done = bf16[80,2560]{1,0:T(8,128)(2,1)} async-done(((bf16[2560,2560]{1,0:T(8,128)(2,1)}), bf16[80,2560]{1,0:T(8,128)(2,1)}) %reduce-scatter.2.cloned.1.call-update) | async-done | bytes 409616 | tf_op jit(solution)/shard_map/reduce_scatter | solution.py:134
  142.5 9.8 %all-gather.1 = bf16[512,256]{1,0:T(8,128)(2,1)S(1)} all-gather(bf16[128,256]{1,0:T(8,128)(2,1)S(1)} %copy-done.3), channel_id=3, replica_groups=mesh['dp'=32,'tensor'=4] {'tensor'}, dimensions={0}, use_global_device_ids=true | all-gather | bytes 327680 | tf_op jit(solution)/shard_map/all_gather | solution.py:92
  152.3 2.3 fusion.2
  154.6 10.1 %all-to-all-start = ((bf16[32,8,2560]{2,1,0:T(8,128)(2,1)}), bf16[32,8,2560]{2,1,0:T(8,128)(2,1)S(1)}, u32[]{:S(2)}, u32[]{:S(2)}) async-start(bf16[32,8,2560]{2,1,0:T(8,128)(2,1)} %fusion.2), calls=%async_computation.1 | async-start | bytes 2621440 | tf_op jit(solution)/shard_map/all_to_all | solution.py:102
  164.7 19.3 %all-to-all-done = bf16[32,8,2560]{2,1,0:T(8,128)(2,1)S(1)} async-done(((bf16[32,8,2560]{2,1,0:T(8,128)(2,1)}), bf16[32,8,2560]{2,1,0:T(8,128)(2,1)S(1)}, u32[]{:S(2)}, u32[]{:S(2)}) %all-to-all-start) | async-done | bytes 1310752 | tf_op jit(solution)/shard_map/all_to_all | solution.py:102
  185.1 1.8 broadcast_in_dim.10
  186.9 5.5 %all-to-all-start.1 = ((f32[32,8,2560]{2,1,0:T(8,128)}), f32[32,8,2560]{2,1,0:T(8,128)S(1)}, u32[]{:S(2)}, u32[]{:S(2)}) async-start(f32[32,8,2560]{2,1,0:T(8,128)} %broadcast_in_dim.10), calls=%async_computation.2 | async-start | bytes 5242880 | tf_op jit(solution)/shard_map/all_to_all | solution.py:110
  194.9 46.6 %all-to-all-done.1 = f32[32,8,2560]{2,1,0:T(8,128)S(1)} async-done(((f32[32,8,2560]{2,1,0:T(8,128)}), f32[32,8,2560]{2,1,0:T(8,128)S(1)}, u32[]{:S(2)}, u32[]{:S(2)}) %all-to-all-start.1) | async-done | bytes 2621472 | tf_op jit(solution)/shard_map/all_to_all | solution.py:110
  242.0 1.4 fusion.29
  243.6 1.6 convolution_add_fusion.4
  245.2 1.4 fusion.45
  246.8 1.6 convolution_add_fusion.3
  248.4 1.4 fusion.46
  250.0 1.5 convolution_add_fusion.2
  251.6 1.4 fusion.47
  253.2 1.5 convolution_add_fusion.1
  254.8 1.7 fusion.48
  256.7 2.7 fusion.1
  259.4 1.6 copy.25
  261.0 8.6 %shard_map.128 = bf16[30,64,2560]{2,1,0:T(8,128)(2,1)} custom-call(s32[30]{0:T(128)} %broadcast_clamp_fusion.index_ref, bf16[32,80,2560]{2,1,0:T(8,128)(2,1)} %bitcast.117), custom_call_target="tpu_custom_call" | custom-call | bytes 19660800 | tf_op jit(solution)/shard_map/pallas_call | solution.py:52
  269.6 1.5 dynamic-slice_bitcast_fusion
  271.2 1.5 copy.31
  (77 shorter events, 21.7 us)
Async XLA Ops:
  7.2 122.3 %reduce-scatter.2.cloned.1.call-start = ((), (), s32[]{:S(2)}) async-start(), calls=%async_computation.3 | async-start | bytes 13516800 | tf_op jit(solution)/shard_map/reduce_scatter | solution.py:134
  14.1 1.1 copy-start
  14.2 1.3 copy-start.2
  22.1 107.5 %copy-start.1 = (f32[1,74,2560]{2,0,1:T(1,128)S(1)}, f32[1,74,2560]{2,0,1:T(1,128)}, u32[]{:S(2)}) copy-start(f32[1,74,2560]{2,0,1:T(1,128)} %param.16) | copy-start | bytes 2273284
  22.1 239.0 %all-gather.4.cloned.1.call-start = ((), (), s32[]{:S(2)}) async-start(), calls=%async_computation.4 | async-start | bytes 13516800 | tf_op jit(solution)/shard_map/all_gather | solution.py:148
  139.9 2.6 copy-start.3
  154.6 29.4 %all-to-all-start = ((bf16[32,8,2560]{2,1,0:T(8,128)(2,1)}), bf16[32,8,2560]{2,1,0:T(8,128)(2,1)S(1)}, u32[]{:S(2)}, u32[]{:S(2)}) async-start(bf16[32,8,2560]{2,1,0:T(8,128)(2,1)} %fusion.2), calls=%async_computation.1 | async-start | bytes 2621440 | tf_op jit(solution)/shard_map/all_to_all | solution.py:102
  186.9 7.4 %copy-start.4 = (s32[1,31]{1,0:T(1,128)S(1)}, s32[1,31]{1,0:T(1,128)}, u32[]{:S(2)}) copy-start(s32[1,31]{1,0:T(1,128)} %param.15) | copy-start | bytes 376
  186.9 54.5 %all-to-all-start.1 = ((f32[32,8,2560]{2,1,0:T(8,128)}), f32[32,8,2560]{2,1,0:T(8,128)S(1)}, u32[]{:S(2)}, u32[]{:S(2)}) async-start(f32[32,8,2560]{2,1,0:T(8,128)} %broadcast_in_dim.10), calls=%async_computation.2 | async-start | bytes 5242880 | tf_op jit(solution)/shard_map/all_to_all | solution.py:110
Sparse Core Ops, SparseCore 0:
  22.2 107.2 reduce-scatter.1
  142.6 101.1 all-gather.3

commit v4 on v3

--- a/solution.py
+++ b/solution.py
@@ -131,8 +131,9 @@
     )
     factors = jnp.concatenate([layer_input, out_grad], axis=0)
     send = lax.dot_general(send_cols, factors, contract, preferred_element_type=f32).astype(bf16)
-    owned = lax.psum_scatter(send, "dp", scatter_dimension=0, tiled=True).astype(f32)
-    owned_sum = owned[:capacity]
+    owned = lax.psum_scatter(send, "dp", scatter_dimension=0, tiled=True)
+    owned, bc_update = lax.optimization_barrier((owned, bc_update))
+    owned_sum = owned[:capacity].astype(f32)
 
     moment = momentum_decay * head_momentum[0] + owned_sum
     head_direction = orthogonalize(moment[None, :HD])[0]

time: 282 us -> 251 us (0.89)
  waiting for transfers between devices: 173 us -> 86.4 us
  blocking collectives: 9.8 us -> 73.5 us
  starting transfers between devices: 15.7 us -> 9.79 us
    reduce_scatter x1, waiting for transfers between devices: 107 us -> 5.94 us  [on_device(): owned = lax.psum_scatter(send, 'dp', scatter_dimension=0, tiled=True)]
    all_gather x1, waiting for transfers between devices: 0.01 us -> 61.2 us  [on_device(): everything = lax.all_gather(owned_update, 'dp', axis=0, tiled=False)]
    all_to_all x0 -> x1, blocking collectives: none -> 61.2 us  [on_device(): lax.all_to_all(bc_copies, 'dp', split_axis=0, concat_axis=0, tiled=True)]
    all_to_all x1 -> x0, waiting for transfers between devices: 46.6 us -> none  [on_device(): lax.all_to_all(bc_copies, 'dp', split_axis=0, concat_axis=0, tiled=True)]
    all_to_all x1 -> x0, starting transfers between devices: 5.49 us -> none  [on_device(): lax.all_to_all(bc_copies, 'dp', split_axis=0, concat_axis=0, tiled=True)]
    unnamed x14 -> x12, local copies, waits for them, and re-layouts: 5.76 us -> 6.57 us
  transfers between devices with their start and end apart: 4 -> 3, of which waited for: 3 -> 3; matrix products, arithmetic and copies ran while one was open for 9% -> 9% of each run, Pallas kernels for 0% -> 0%
where the time goes in v4:
time: 251 us; the launch traced here: 250 us
  waiting for transfers between devices  86.4 us (34%)
  blocking collectives  73.5 us (29%)
  matrix products  34.6 us (14%)
  between operations  17.7 us (7%)
  local copies, waits for them, and re-layouts  12.7 us (5%)
  starting transfers between devices  9.79 us (4%)
  Pallas kernels  8.58 us (3%)
  other arithmetic  6.69 us (3%)
    all_gather x1, waiting for transfers between devices, on_device(): everything = lax.all_gather(owned_update, 'dp', axis=0, tiled=False)  61.2 us
    all_to_all x1, blocking collectives, on_device(): lax.all_to_all(bc_copies, 'dp', split_axis=0, concat_axis=0, tiled=True)  61.2 us
    all_to_all x1, waiting for transfers between devices, on_device(): lax.all_to_all(bc_part, 'dp', split_axis=0, concat_axis=0, tiled=True)  19.2 us
    all_gather x1, blocking collectives, on_device(): lax.all_gather(bc_grad, 'tensor', axis=0).astype(f32)  12.3 us
    dot_general x15, matrix products, orthogonalize(): jnp.einsum('bij,bjk->bik', polynomial, current, precision=highest)  12.3 us
    dot_general x15, matrix products, orthogonalize(): jnp.einsum('bik,bjk->bij', current, current, precision=highest)  10.4 us
    all_to_all x1, starting transfers between devices, on_device(): lax.all_to_all(bc_part, 'dp', split_axis=0, concat_axis=0, tiled=True)  9.71 us
    pallas_call x1, Pallas kernels, gather_slabs(): pl.pallas_call(_gather_kernel, grid_spec=pltpu.PrefetchScalarGridSpec(num...  8.58 us
  transfers between devices with their start and end apart: 3, of which 3 were waited for; matrix products, arithmetic and copies ran while one was open for 9% of the time, Pallas kernels for 0%

profile of v4, /device:TPU:1, one launch (start us, length us, event | category | flops | bytes accessed | tf_op | source)
XLA Modules:
  0.0 250.0 jit_solution(12386639608958626733)
XLA Ops:
  7.2 1.2 slice.21
  15.4 6.6 %convolution_convert_fusion = bf16[2560,2560]{1,0:T(8,128)(2,1)} fusion(bf16[256,2560]{0,1:T(8,128)(2,1)S(1)} %bitcast.121, bf16[128,2560]{1,0:T(8,128)(2,1)S(1)} %copy-done.1, bf16[128,2560]{1,0:T(8,128)(2,1)S(1)} %copy-done), kind=kOutput, calls=%fused_computation | convolution fusion | flops 3364618240 | bytes 15728640 | tf_op jit(solution)/shard_map/dot_general | solution.py:133
  22.9 12.3 %all-gather = bf16[512,256]{1,0:T(8,128)(2,1)S(1)} all-gather(bf16[128,256]{1,0:T(8,128)(2,1)S(1)} %copy-done.2), channel_id=2, replica_groups=mesh['dp'=32,'tensor'=4] {'tensor'}, dimensions={0}, use_global_device_ids=true | all-gather | bytes 327680 | tf_op jit(solution)/shard_map/all_gather | solution.py:92
  35.2 2.3 fusion.2
  37.5 9.7 %all-to-all-start = ((bf16[32,8,2560]{2,1,0:T(8,128)(2,1)}), bf16[32,8,2560]{2,1,0:T(8,128)(2,1)S(1)}, u32[]{:S(2)}, u32[]{:S(2)}) async-start(bf16[32,8,2560]{2,1,0:T(8,128)(2,1)} %fusion.2), calls=%async_computation.1 | async-start | bytes 2621440 | tf_op jit(solution)/shard_map/all_to_all | solution.py:102
  47.3 19.2 %all-to-all-done = bf16[32,8,2560]{2,1,0:T(8,128)(2,1)S(1)} async-done(((bf16[32,8,2560]{2,1,0:T(8,128)(2,1)}), bf16[32,8,2560]{2,1,0:T(8,128)(2,1)S(1)}, u32[]{:S(2)}, u32[]{:S(2)}) %all-to-all-start) | async-done | bytes 1310752 | tf_op jit(solution)/shard_map/all_to_all | solution.py:102
  67.9 61.2 %all_to_all.14 = f32[32,8,2560]{2,1,0:T(8,128)S(1)} all-to-all(f32[32,8,2560]{2,1,0:T(8,128)S(1)} %broadcast_in_dim.9), channel_id=1, replica_groups=mesh['dp'=32,'tensor'=4] {'dp'}, dimensions={0} | all-to-all | bytes 5242880 | tf_op jit(solution)/shard_map/all_to_all | solution.py:110
  129.6 1.4 fusion.29
  131.3 1.6 convolution_add_fusion.4
  132.8 1.4 fusion.37
  134.5 1.5 convolution_add_fusion.3
  136.0 1.4 fusion.38
  137.7 1.5 convolution_add_fusion.2
  139.2 1.4 fusion.39
  140.9 1.5 convolution_add_fusion.1
  142.4 1.7 fusion.40
  144.3 2.7 %fusion.1 = bf16[2,128,2560]{2,1,0:T(8,128)(2,1)} fusion(f32[2,128,128]{2,1,0:T(8,128)S(1)} %fusion.11, f32[2,128,2560]{2,1,0:T(8,128)S(1)} %convolution_add_fusion.1), kind=kOutput, calls=%fused_computation.8 | convolution fusion | flops 505937920 | bytes 4063232 | tf_op jit(solution)/shard_map/bij,bjk->bik/dot_general | solution.py:29
  147.0 5.9 %reduce-scatter.2.cloned.1.call-done = bf16[80,2560]{1,0:T(8,128)(2,1)} async-done(((bf16[2560,2560]{1,0:T(8,128)(2,1)}), bf16[80,2560]{1,0:T(8,128)(2,1)}) %reduce-scatter.2.cloned.1.call-update) | async-done | bytes 409616 | tf_op jit(solution)/shard_map/reduce_scatter | solution.py:134
  152.9 1.3 bitcast_add_fusion
  168.6 1.6 copy.25
  170.3 61.2 %all-gather.4.cloned.1.call-done = bf16[2560,2560]{1,0:T(8,128)(2,1)} async-done(((bf16[80,2560]{1,0:T(8,128)(2,1)}), bf16[2560,2560]{1,0:T(8,128)(2,1)}) %all-gather.4.cloned.1.call-update) | async-done | bytes 13107216 | tf_op jit(solution)/shard_map/all_gather | solution.py:149
  231.5 1.5 dynamic-slice_bitcast_fusion
  233.0 8.6 %shard_map.128 = bf16[30,64,2560]{2,1,0:T(8,128)(2,1)} custom-call(s32[30]{0:T(128)} %broadcast_clamp_fusion.index_ref, bf16[32,80,2560]{2,1,0:T(8,128)(2,1)} %bitcast.118), custom_call_target="tpu_custom_call" | custom-call | bytes 19660800 | tf_op jit(solution)/shard_map/pallas_call | solution.py:52
  241.6 1.5 copy.31
  (74 shorter events, 21.7 us)
Async XLA Ops:
  7.2 145.8 %reduce-scatter.2.cloned.1.call-start = ((), (), s32[]{:S(2)}) async-start(), calls=%async_computation.3 | async-start | bytes 13516800 | tf_op jit(solution)/shard_map/reduce_scatter | solution.py:134
  14.1 1.1 copy-start
  14.1 1.3 copy-start.1
  22.0 0.8 copy-start.2
  37.5 29.0 %all-to-all-start = ((bf16[32,8,2560]{2,1,0:T(8,128)(2,1)}), bf16[32,8,2560]{2,1,0:T(8,128)(2,1)S(1)}, u32[]{:S(2)}, u32[]{:S(2)}) async-start(bf16[32,8,2560]{2,1,0:T(8,128)(2,1)} %fusion.2), calls=%async_computation.1 | async-start | bytes 2621440 | tf_op jit(solution)/shard_map/all_to_all | solution.py:102
  47.2 184.3 %all-gather.4.cloned.1.call-start = ((), (), s32[]{:S(2)}) async-start(), calls=%async_computation.4 | async-start | bytes 13516800 | tf_op jit(solution)/shard_map/all_gather | solution.py:149
  163.6 4.5 %copy-start.3 = (s32[1,31]{1,0:T(1,128)S(1)}, s32[1,31]{1,0:T(1,128)}, u32[]{:S(2)}) copy-start(s32[1,31]{1,0:T(1,128)} %param.15) | copy-start | bytes 376
Sparse Core Ops, SparseCore 0:
  22.2 130.7 reduce-scatter.1
  166.2 65.2 all-gather.3

commit v5 on v4

--- a/solution.py
+++ b/solution.py
@@ -91,9 +91,13 @@
 
     bc_cols = jnp.sum(lax.all_gather(bc_grad, "tensor", axis=0).astype(f32), axis=0)
     bc_total = bc_cols.shape[1]
-    bc_rows = bc_total // n_data
+    n_tensor = lax.axis_size("tensor")
+    plane = lax.axis_index("tensor")
+    plane_rows = bc_total // n_tensor
+    bc_rows = plane_rows // n_data
+    plane_cols = lax.dynamic_slice_in_dim(bc_cols, plane * plane_rows, plane_rows, axis=1)
     bc_part = lax.dot_general(
-        bc_cols,
+        plane_cols,
         layer_input.astype(f32),
         contract,
         precision=lax.Precision.HIGHEST,
@@ -104,10 +108,13 @@
     me = lax.axis_index("dp")
     bc_flat = bc_momentum.reshape(bc_total, width)
     bc_moment_rows = momentum_decay * lax.dynamic_slice_in_dim(
-        bc_flat, me * bc_rows, bc_rows, axis=0
+        bc_flat, plane * plane_rows + me * bc_rows, bc_rows, axis=0
     ) + bc_sum_rows
     bc_copies = jnp.broadcast_to(bc_moment_rows[None], (n_data, bc_rows, width))
-    bc_moment = lax.all_to_all(bc_copies, "dp", split_axis=0, concat_axis=0, tiled=True)
+    plane_moment = lax.all_to_all(bc_copies, "dp", split_axis=0, concat_axis=0, tiled=True)
+    plane_moment = plane_moment.reshape(plane_rows, width)
+    plane_copies = jnp.broadcast_to(plane_moment[None], (n_tensor, plane_rows, width))
+    bc_moment = lax.all_to_all(plane_copies, "tensor", split_axis=0, concat_axis=0, tiled=True)
     bc_moment = bc_moment.reshape(2, STATE, width)
     scale = math.sqrt(width)
     bc_update = (orthogonalize(bc_moment) * scale).astype(bf16)

time: 251 us -> 227 us (0.904)
  waiting for transfers between devices: 86.4 us -> 72.9 us
  blocking collectives: 73.5 us -> 63.6 us
    all_to_all x1, blocking collectives: 61.2 us -> 16.3 us  [on_device(): lax.all_to_all(bc_copies, 'dp', split_axis=0, concat_axis=0, tiled=True)]
    all_to_all x0 -> x1, blocking collectives: none -> 34.9 us  [on_device(): lax.all_to_all(plane_copies, 'tensor', split_axis=0, concat_axis=0, tiled...]
    all_to_all x1, waiting for transfers between devices: 19.2 us -> 9.45 us  [on_device(): lax.all_to_all(bc_part, 'dp', split_axis=0, concat_axis=0, tiled=True)]
    reduce_scatter x1, waiting for transfers between devices: 5.94 us -> 1.87 us  [on_device(): owned = lax.psum_scatter(send, 'dp', scatter_dimension=0, tiled=True)]
  transfers between devices with their start and end apart: 3 -> 3, of which waited for: 3 -> 3; matrix products, arithmetic and copies ran while one was open for 9% -> 10% of each run, Pallas kernels for 0% -> 0%
where the time goes in v5:
time: 227 us; the launch traced here: 226 us
  waiting for transfers between devices  72.9 us (32%)
  blocking collectives  63.6 us (28%)
  matrix products  32.9 us (14%)
  between operations  17.8 us (8%)
  local copies, waits for them, and re-layouts  14.1 us (6%)
  starting transfers between devices  9.79 us (4%)
  Pallas kernels  8.58 us (4%)
  other arithmetic  6.79 us (3%)
    all_gather x1, waiting for transfers between devices, on_device(): everything = lax.all_gather(owned_update, 'dp', axis=0, tiled=False)  61.5 us
    all_to_all x1, blocking collectives, on_device(): lax.all_to_all(plane_copies, 'tensor', split_axis=0, concat_axis=0, tiled...  34.9 us
    all_to_all x1, blocking collectives, on_device(): lax.all_to_all(bc_copies, 'dp', split_axis=0, concat_axis=0, tiled=True)  16.3 us
    dot_general x15, matrix products, orthogonalize(): jnp.einsum('bij,bjk->bik', polynomial, current, precision=highest)  12.5 us
    all_gather x1, blocking collectives, on_device(): lax.all_gather(bc_grad, 'tensor', axis=0).astype(f32)  12.3 us
    dot_general x15, matrix products, orthogonalize(): jnp.einsum('bik,bjk->bij', current, current, precision=highest)  10.3 us
    all_to_all x1, starting transfers between devices, on_device(): lax.all_to_all(bc_part, 'dp', split_axis=0, concat_axis=0, tiled=True)  9.71 us
    all_to_all x1, waiting for transfers between devices, on_device(): lax.all_to_all(bc_part, 'dp', split_axis=0, concat_axis=0, tiled=True)  9.45 us
  transfers between devices with their start and end apart: 3, of which 3 were waited for; matrix products, arithmetic and copies ran while one was open for 10% of the time, Pallas kernels for 0%

profile of v5, /device:TPU:1, one launch (start us, length us, event | category | flops | bytes accessed | tf_op | source)
XLA Modules:
  0.0 226.5 jit_solution(17172023236250854592)
XLA Ops:
  7.2 1.2 slice.21
  15.4 6.6 %convolution_convert_fusion = bf16[2560,2560]{1,0:T(8,128)(2,1)} fusion(bf16[256,2560]{0,1:T(8,128)(2,1)S(1)} %bitcast.118, bf16[128,2560]{1,0:T(8,128)(2,1)S(1)} %copy-done.1, bf16[128,2560]{1,0:T(8,128)(2,1)S(1)} %copy-done), kind=kOutput, calls=%fused_computation | convolution fusion | flops 3364618240 | bytes 15728640 | tf_op jit(solution)/shard_map/dot_general | solution.py:140
  22.9 12.3 %all-gather = bf16[512,256]{1,0:T(8,128)(2,1)S(1)} all-gather(bf16[128,256]{1,0:T(8,128)(2,1)S(1)} %copy-done.2), channel_id=2, replica_groups=mesh['dp'=32,'tensor'=4] {'tensor'}, dimensions={0}, use_global_device_ids=true | all-gather | bytes 327680 | tf_op jit(solution)/shard_map/all_gather | solution.py:92
  36.6 9.7 %all-to-all-start = ((bf16[32,2,2560]{2,1,0:T(2,128)(2,1)}), bf16[32,2,2560]{2,1,0:T(2,128)(2,1)S(1)}, u32[]{:S(2)}, u32[]{:S(2)}) async-start(bf16[32,2,2560]{2,1,0:T(2,128)(2,1)} %all_to_all.12), calls=%async_computation.1 | async-start | bytes 655360 | tf_op jit(solution)/shard_map/all_to_all | solution.py:106
  46.4 9.5 %all-to-all-done = bf16[32,2,2560]{2,1,0:T(2,128)(2,1)S(1)} async-done(((bf16[32,2,2560]{2,1,0:T(2,128)(2,1)}), bf16[32,2,2560]{2,1,0:T(2,128)(2,1)S(1)}, u32[]{:S(2)}, u32[]{:S(2)}) %all-to-all-start) | async-done | bytes 327712 | tf_op jit(solution)/shard_map/all_to_all | solution.py:106
  57.3 16.3 %all_to_all.19 = f32[32,2,2560]{2,1,0:T(2,128)S(1)} all-to-all(f32[32,2,2560]{2,1,0:T(2,128)S(1)} %broadcast_in_dim.13), channel_id=1, replica_groups=mesh['dp'=32,'tensor'=4] {'dp'}, dimensions={0} | all-to-all | bytes 1310720 | tf_op jit(solution)/shard_map/all_to_all | solution.py:114
  74.3 34.9 %all_to_all.20 = f32[4,64,2560]{2,1,0:T(8,128)S(1)} all-to-all(f32[4,64,2560]{2,1,0:T(8,128)S(1)} %broadcast_in_dim.15), channel_id=1, replica_groups=mesh['dp'=32,'tensor'=4] {'tensor'}, dimensions={0} | all-to-all | bytes 5242880 | tf_op jit(solution)/shard_map/all_to_all | solution.py:117
  109.8 1.4 fusion.28
  111.5 1.6 convolution_add_fusion.4
  113.1 1.4 fusion.38
  114.7 1.6 convolution_add_fusion.3
  116.3 1.4 fusion.39
  117.9 1.6 convolution_add_fusion.2
  119.5 1.4 fusion.40
  121.1 1.6 convolution_add_fusion.1
  122.7 1.6 fusion.41
  124.5 2.7 %fusion.1 = bf16[2,128,2560]{2,1,0:T(8,128)(2,1)} fusion(f32[2,128,128]{2,1,0:T(8,128)S(1)} %fusion.10, f32[2,128,2560]{2,1,0:T(8,128)S(1)} %convolution_add_fusion.1), kind=kOutput, calls=%fused_computation.7 | convolution fusion | flops 505937920 | bytes 4063232 | tf_op jit(solution)/shard_map/bij,bjk->bik/dot_general | solution.py:29
  127.2 1.9 reduce-scatter.2.cloned.1.call-done
  129.1 1.3 bitcast_add_fusion
  144.8 1.6 copy.25
  146.5 61.5 %all-gather.4.cloned.1.call-done = bf16[2560,2560]{1,0:T(8,128)(2,1)} async-done(((bf16[80,2560]{1,0:T(8,128)(2,1)}), bf16[2560,2560]{1,0:T(8,128)(2,1)}) %all-gather.4.cloned.1.call-update) | async-done | bytes 13107216 | tf_op jit(solution)/shard_map/all_gather | solution.py:156
  208.0 1.5 dynamic-slice_bitcast_fusion
  209.5 8.6 %shard_map.128 = bf16[30,64,2560]{2,1,0:T(8,128)(2,1)} custom-call(s32[30]{0:T(128)} %broadcast_clamp_fusion.index_ref, bf16[32,80,2560]{2,1,0:T(8,128)(2,1)} %bitcast.115), custom_call_target="tpu_custom_call" | custom-call | bytes 19660800 | tf_op jit(solution)/shard_map/pallas_call | solution.py:52
  218.1 1.5 copy.31
  (78 shorter events, 23.8 us)
Async XLA Ops:
  7.2 122.0 %reduce-scatter.2.cloned.1.call-start = ((), (), s32[]{:S(2)}) async-start(), calls=%async_computation.4 | async-start | bytes 13516800 | tf_op jit(solution)/shard_map/reduce_scatter | solution.py:141
  14.1 1.1 copy-start
  14.1 1.3 copy-start.1
  22.0 0.8 copy-start.2
  36.6 19.2 %all-to-all-start = ((bf16[32,2,2560]{2,1,0:T(2,128)(2,1)}), bf16[32,2,2560]{2,1,0:T(2,128)(2,1)S(1)}, u32[]{:S(2)}, u32[]{:S(2)}) async-start(bf16[32,2,2560]{2,1,0:T(2,128)(2,1)} %all_to_all.12), calls=%async_computation.1 | async-start | bytes 655360 | tf_op jit(solution)/shard_map/all_to_all | solution.py:106
  46.4 161.6 %all-gather.4.cloned.1.call-start = ((), (), s32[]{:S(2)}) async-start(), calls=%async_computation.5 | async-start | bytes 13516800 | tf_op jit(solution)/shard_map/all_gather | solution.py:156
  139.7 4.5 %copy-start.3 = (s32[1,31]{1,0:T(1,128)S(1)}, s32[1,31]{1,0:T(1,128)}, u32[]{:S(2)}) copy-start(s32[1,31]{1,0:T(1,128)} %param.15) | copy-start | bytes 376
Sparse Core Ops, SparseCore 0:
  22.2 106.8 reduce-scatter.1
  142.4 65.5 all-gather.3

commit v6 on v5

--- a/solution.py
+++ b/solution.py
@@ -103,19 +103,25 @@
         precision=lax.Precision.HIGHEST,
         preferred_element_type=f32,
     ).astype(bf16)
-    bc_pieces = lax.all_to_all(bc_part, "dp", split_axis=0, concat_axis=0, tiled=True)
-    bc_sum_rows = jnp.sum(bc_pieces.reshape(n_data, bc_rows, width).astype(f32), axis=0)
+    dt_part = lax.dot_general(dt_grad, layer_input, contract, preferred_element_type=f32).astype(bf16)
+    outgoing = jnp.concatenate(
+        [
+            bc_part.reshape(n_data, bc_rows, width),
+            jnp.broadcast_to(dt_part[None], (n_data, heads_here, width)),
+        ],
+        axis=1,
+    )
+    incoming = lax.all_to_all(outgoing, "dp", split_axis=0, concat_axis=0, tiled=True)
+    incoming_sum = jnp.sum(incoming.astype(f32), axis=0)
+    bc_sum_rows = incoming_sum[:bc_rows]
+    dt_sum = incoming_sum[bc_rows:]
     me = lax.axis_index("dp")
-    bc_flat = bc_momentum.reshape(bc_total, width)
-    bc_moment_rows = momentum_decay * lax.dynamic_slice_in_dim(
-        bc_flat, plane * plane_rows + me * bc_rows, bc_rows, axis=0
-    ) + bc_sum_rows
-    bc_copies = jnp.broadcast_to(bc_moment_rows[None], (n_data, bc_rows, width))
-    plane_moment = lax.all_to_all(bc_copies, "dp", split_axis=0, concat_axis=0, tiled=True)
-    plane_moment = plane_moment.reshape(plane_rows, width)
-    plane_copies = jnp.broadcast_to(plane_moment[None], (n_tensor, plane_rows, width))
-    bc_moment = lax.all_to_all(plane_copies, "tensor", split_axis=0, concat_axis=0, tiled=True)
-    bc_moment = bc_moment.reshape(2, STATE, width)
+    bc_copies = jnp.broadcast_to(bc_sum_rows.astype(bf16)[None], (n_data, bc_rows, width))
+    plane_sum = lax.all_to_all(bc_copies, "dp", split_axis=0, concat_axis=0, tiled=True)
+    plane_sum = plane_sum.reshape(plane_rows, width)
+    plane_copies = jnp.broadcast_to(plane_sum[None], (n_tensor, plane_rows, width))
+    bc_sum = lax.all_to_all(plane_copies, "tensor", split_axis=0, concat_axis=0, tiled=True)
+    bc_moment = momentum_decay * bc_momentum + bc_sum.astype(f32).reshape(2, STATE, width)
     scale = math.sqrt(width)
     bc_update = (orthogonalize(bc_moment) * scale).astype(bf16)
 
@@ -125,26 +131,20 @@
     lower = jnp.concatenate([jnp.zeros_like(zx), io], axis=2).reshape(tokens, n_blocks, HD)
     grad_blocks = jnp.concatenate([upper, lower], axis=0)
     pick = (head_owner[None, :] == slots[:, None]).astype(bf16)
-    owner_cols = jnp.einsum(
+    send_cols = jnp.einsum(
         "tbr,ob->tor", grad_blocks, pick, preferred_element_type=f32
-    ).astype(bf16)
-    dt_cols = jnp.concatenate([dt_grad, jnp.zeros_like(dt_grad)], axis=0)
-    is_dt = (slots == dt_owner).astype(bf16)
-    dt_owner_cols = dt_cols[:, None, :] * is_dt[None, :, None]
-    chunk = -(-capacity // 16) * 16
-    pad_cols = jnp.zeros((2 * tokens, n_data, chunk - capacity), bf16)
-    send_cols = jnp.concatenate([owner_cols, dt_owner_cols, pad_cols], axis=2).reshape(
-        2 * tokens, n_data * chunk
-    )
+    ).astype(bf16).reshape(2 * tokens, n_data * HD)
     factors = jnp.concatenate([layer_input, out_grad], axis=0)
     send = lax.dot_general(send_cols, factors, contract, preferred_element_type=f32).astype(bf16)
     owned = lax.psum_scatter(send, "dp", scatter_dimension=0, tiled=True)
-    owned, bc_update = lax.optimization_barrier((owned, bc_update))
-    owned_sum = owned[:capacity].astype(f32)
+    owned, bc_update, dt_sum = lax.optimization_barrier((owned, bc_update, dt_sum))
+    dt_rows = jnp.where(me == dt_owner, dt_sum, jnp.zeros_like(dt_sum))
+    owned_sum = jnp.concatenate([owned.astype(f32), dt_rows], axis=0)
 
     moment = momentum_decay * head_momentum[0] + owned_sum
     head_direction = orthogonalize(moment[None, :HD])[0]
     dt_direction = orthogonalize(moment[None, HD:])[0]
+    chunk = -(-capacity // 16) * 16
     owned_update = jnp.concatenate(
         [
             (head_direction * scale).astype(bf16),

time: 227 us -> 230 us (1.013)
  blocking collectives: 63.6 us -> 72 us
  starting transfers between devices: 9.79 us -> 4.21 us
  local copies, waits for them, and re-layouts: 14.1 us -> 10.9 us
    all_to_all x1, blocking collectives: 34.9 us -> 43.4 us  [on_device(): lax.all_to_all(outgoing, 'dp', split_axis=0, concat_axis=0, tiled=True)]
    all_to_all x1, waiting for transfers between devices: 9.45 us -> 15.2 us  [on_device(): lax.all_to_all(plane_copies, 'tensor', split_axis=0, concat_axis=0, tiled...]
    all_to_all x1, starting transfers between devices: 9.71 us -> 4.17 us  [on_device(): lax.all_to_all(plane_copies, 'tensor', split_axis=0, concat_axis=0, tiled...]
    all_gather x1, waiting for transfers between devices: 61.5 us -> 58.6 us  [on_device(): everything = lax.all_gather(owned_update, 'dp', axis=0, tiled=False)]
    unnamed x12 -> x19, local copies, waits for them, and re-layouts: 6.56 us -> 4.76 us
  transfers between devices with their start and end apart: 3 -> 3, of which waited for: 3 -> 2; matrix products, arithmetic and copies ran while one was open for 10% -> 12% of each run, Pallas kernels for 0% -> 0%
where the time goes in v6:
time: 230 us; the launch traced here: 229 us
  waiting for transfers between devices  73.8 us (32%)
  blocking collectives  72 us (31%)
  matrix products  32.1 us (14%)
  between operations  18.5 us (8%)
  local copies, waits for them, and re-layouts  10.9 us (5%)
  other arithmetic  9.02 us (4%)
  Pallas kernels  8.71 us (4%)
  starting transfers between devices  4.21 us (2%)
    all_gather x1, waiting for transfers between devices, on_device(): everything = lax.all_gather(owned_update, 'dp', axis=0, tiled=False)  58.6 us
    all_to_all x1, blocking collectives, on_device(): lax.all_to_all(outgoing, 'dp', split_axis=0, concat_axis=0, tiled=True)  43.4 us
    all_to_all x1, blocking collectives, on_device(): lax.all_to_all(bc_copies, 'dp', split_axis=0, concat_axis=0, tiled=True)  16.3 us
    all_to_all x1, waiting for transfers between devices, on_device(): lax.all_to_all(plane_copies, 'tensor', split_axis=0, concat_axis=0, tiled...  15.2 us
    dot_general x15, matrix products, orthogonalize(): jnp.einsum('bij,bjk->bik', polynomial, current, precision=highest)  12.4 us
    all_gather x1, blocking collectives, on_device(): lax.all_gather(bc_grad, 'tensor', axis=0).astype(f32)  12.3 us
    dot_general x15, matrix products, orthogonalize(): jnp.einsum('bik,bjk->bij', current, current, precision=highest)  10.3 us
    pallas_call x1, Pallas kernels, gather_slabs(): pl.pallas_call(_gather_kernel, grid_spec=pltpu.PrefetchScalarGridSpec(num...  8.71 us
  transfers between devices with their start and end apart: 3, of which 2 were waited for; matrix products, arithmetic and copies ran while one was open for 12% of the time, Pallas kernels for 0%

profile of v6, /device:TPU:1, one launch (start us, length us, event | category | flops | bytes accessed | tf_op | source)
XLA Modules:
  0.0 229.3 jit_solution(8161350727099212805)
XLA Ops:
  9.4 1.2 copy.45
  12.0 5.6 %convolution_convert_fusion = bf16[2048,2560]{1,0:T(8,128)(2,1)} fusion(bf16[256,2048]{0,1:T(8,128)(2,1)S(1)} %bitcast.122, bf16[128,2560]{1,0:T(8,128)(2,1)S(1)} %copy-done.5, bf16[128,2560]{1,0:T(8,128)(2,1)S(1)} %copy-done.2), kind=kOutput, calls=%fused_computation | convolution fusion | flops 2692218880 | bytes 12845056 | tf_op jit(solution)/shard_map/dot_general | solution.py:138
  18.5 12.3 %all-gather = bf16[512,256]{1,0:T(8,128)(2,1)S(1)} all-gather(bf16[128,256]{1,0:T(8,128)(2,1)S(1)} %copy-done.6), channel_id=2, replica_groups=mesh['dp'=32,'tensor'=4] {'tensor'}, dimensions={0}, use_global_device_ids=true | all-gather | bytes 327680 | tf_op jit(solution)/shard_map/all_gather | solution.py:92
  33.1 43.4 %all_to_all.15 = bf16[32,12,2560]{2,1,0:T(8,128)(2,1)S(1)} all-to-all(bf16[32,12,2560]{2,1,0:T(8,128)(2,1)S(1)} %pad_maximum_fusion), channel_id=1, replica_groups=mesh['dp'=32,'tensor'=4] {'dp'}, dimensions={0} | all-to-all | bytes 3932160 | tf_op jit(solution)/shard_map/all_to_all | solution.py:114
  76.5 1.3 convert_reduce_fusion
  78.0 16.3 %all_to_all.16 = bf16[32,2,2560]{2,1,0:T(2,128)(2,1)S(1)} all-to-all(bf16[32,2,2560]{2,1,0:T(2,128)(2,1)S(1)} %broadcast_in_dim.13), channel_id=1, replica_groups=mesh['dp'=32,'tensor'=4] {'dp'}, dimensions={0} | all-to-all | bytes 655360 | tf_op jit(solution)/shard_map/all_to_all | solution.py:120
  94.5 1.2 broadcast_in_dim.15
  95.6 4.2 %all-to-all-start.2 = ((bf16[4,64,2560]{2,1,0:T(8,128)(2,1)}), bf16[4,64,2560]{2,1,0:T(8,128)(2,1)S(1)}, u32[]{:S(2)}, u32[]{:S(2)}) async-start(bf16[4,64,2560]{2,1,0:T(8,128)(2,1)} %broadcast_in_dim.15), calls=%async_computation.3 | async-start | bytes 2621440 | tf_op jit(solution)/shard_map/all_to_all | solution.py:123
  101.1 15.2 %all-to-all-done.2 = bf16[4,64,2560]{2,1,0:T(8,128)(2,1)S(1)} async-done(((bf16[4,64,2560]{2,1,0:T(8,128)(2,1)}), bf16[4,64,2560]{2,1,0:T(8,128)(2,1)S(1)}, u32[]{:S(2)}, u32[]{:S(2)}) %all-to-all-start.2) | async-done | bytes 1310752 | tf_op jit(solution)/shard_map/all_to_all | solution.py:123
  116.3 2.5 %multiply_reduce_fusion = (f32[2]{0:T(128)S(1)}, f32[2,128,2560]{2,1,0:T(8,128)S(1)}) fusion(f32[2,128,2560]{2,1,0:T(8,128)} %param.17, bf16[2,128,2560]{2,1,0:T(8,128)(2,1)S(1)} %bitcast.121), kind=kLoop, calls=%fused_computation.27 | loop fusion | flops 3276798 | bytes 6553608 | tf_op jit(solution)/shard_map/reduce_sum | solution.py:22
  118.8 1.5 fusion.28
  120.5 1.6 convolution_add_fusion.4
  122.1 1.4 fusion.38
  123.7 1.6 convolution_add_fusion.3
  125.3 1.4 fusion.39
  126.9 1.6 convolution_add_fusion.2
  128.5 1.4 fusion.40
  130.1 1.6 convolution_add_fusion.1
  131.7 1.6 fusion.41
  133.6 2.7 %fusion.1 = bf16[2,128,2560]{2,1,0:T(8,128)(2,1)} fusion(f32[2,128,128]{2,1,0:T(8,128)S(1)} %fusion.10, f32[2,128,2560]{2,1,0:T(8,128)S(1)} %convolution_add_fusion.1), kind=kOutput, calls=%fused_computation.8 | convolution fusion | flops 505937920 | bytes 4063232 | tf_op jit(solution)/shard_map/bij,bjk->bik/dot_general | solution.py:29
  151.9 1.6 copy.52
  153.6 58.6 %all-gather.4.cloned.1.call-done = bf16[2560,2560]{1,0:T(8,128)(2,1)} async-done(((bf16[80,2560]{1,0:T(8,128)(2,1)}), bf16[2560,2560]{1,0:T(8,128)(2,1)}) %all-gather.4.cloned.1.call-update) | async-done | bytes 13107216 | tf_op jit(solution)/shard_map/all_gather | solution.py:156
  212.2 1.5 dynamic-slice_bitcast_fusion
  213.7 8.7 %shard_map.128 = bf16[30,64,2560]{2,1,0:T(8,128)(2,1)} custom-call(s32[30]{0:T(128)} %broadcast_clamp_fusion.index_ref, bf16[32,80,2560]{2,1,0:T(8,128)(2,1)} %bitcast.119), custom_call_target="tpu_custom_call" | custom-call | bytes 19660800 | tf_op jit(solution)/shard_map/pallas_call | solution.py:52
  (87 shorter events, 20.9 us)
Async XLA Ops:
  7.2 24.4 %copy-start = (bf16[128,10]{0,1:T(8,128)(2,1)S(1)}, bf16[128,10]{0,1:T(8,128)(2,1)}, u32[]{:S(2)}) copy-start(bf16[128,10]{0,1:T(8,128)(2,1)} %param.14) | copy-start | bytes 7684
  7.2 129.1 %reduce-scatter.2.cloned.1.call-start = ((), (), s32[]{:S(2)}) async-start(), calls=%async_computation.4 | async-start | bytes 10813440 | tf_op jit(solution)/shard_map/reduce_scatter | solution.py:139
  10.6 1.4 copy-start.2
  10.7 1.4 copy-start.5
  17.6 0.8 copy-start.6
  78.0 21.8 %copy-start.7 = (s32[1,31]{1,0:T(1,128)S(1)}, s32[1,31]{1,0:T(1,128)}, u32[]{:S(2)}) copy-start(s32[1,31]{1,0:T(1,128)} %param.15) | copy-start | bytes 376
  95.6 20.7 %all-to-all-start.2 = ((bf16[4,64,2560]{2,1,0:T(8,128)(2,1)}), bf16[4,64,2560]{2,1,0:T(8,128)(2,1)S(1)}, u32[]{:S(2)}, u32[]{:S(2)}) async-start(bf16[4,64,2560]{2,1,0:T(8,128)(2,1)} %broadcast_in_dim.15), calls=%async_computation.3 | async-start | bytes 2621440 | tf_op jit(solution)/shard_map/all_to_all | solution.py:123
  99.8 112.4 %all-gather.4.cloned.1.call-start = ((), (), s32[]{:S(2)}) async-start(), calls=%async_computation.5 | async-start | bytes 13516800 | tf_op jit(solution)/shard_map/all_gather | solution.py:156
  118.8 1.7 copy-start.4
  133.6 3.8 %copy-start.3 = (f32[1,74,2560]{2,0,1:T(1,128)S(1)}, f32[1,74,2560]{2,0,1:T(1,128)}, u32[]{:S(2)}) copy-start(f32[1,74,2560]{2,0,1:T(1,128)} %param.16) | copy-start | bytes 2273284
  213.7 8.7 %copy-start.1 = (bf16[128,10]{0,1:T(8,128)(2,1)S(1)}, bf16[128,10]{0,1:T(8,128)(2,1)}, u32[]{:S(2)}) copy-start(bf16[128,10]{0,1:T(8,128)(2,1)} %param.14) | copy-start | bytes 7684
Sparse Core Ops, SparseCore 0:
  17.8 102.9 reduce-scatter.1
  149.4 62.6 all-gather.3

commit v7 on v5

--- a/solution.py
+++ b/solution.py
@@ -32,36 +32,49 @@
     return current
 
 
-def _gather_kernel(index_ref, source_ref, out_ref, sems):
-    rows = out_ref.shape[1]
+def _gather_kernel(index_ref, source_ref, out_ref, tail_ref, sems):
+    count, rows = out_ref.shape[0], out_ref.shape[1]
+    tail_rows = tail_ref.shape[0]
     copies = []
-    for b in range(out_ref.shape[0]):
-        copy = pltpu.make_async_copy(
-            source_ref.at[index_ref[b], pl.ds(0, rows)], out_ref.at[b], sems.at[b]
+    for b in range(count):
+        copies.append(
+            pltpu.make_async_copy(
+                source_ref.at[index_ref[b], pl.ds(0, rows)], out_ref.at[b], sems.at[b]
+            )
         )
+    copies.append(
+        pltpu.make_async_copy(
+            source_ref.at[index_ref[count], pl.ds(rows, tail_rows)], tail_ref, sems.at[count]
+        )
+    )
+    for copy in copies:
         copy.start()
-        copies.append(copy)
     for copy in copies:
         copy.wait()
 
 
-def gather_slabs(source, index, rows):
-    count = index.shape[0]
+def gather_slabs(source, index, rows, tail_rows):
+    count = index.shape[0] - 1
     n, chunk, width = source.shape
     index = jnp.clip(index, 0, n - 1).astype(jnp.int32)
+    moved = (count * rows + tail_rows) * width * source.dtype.itemsize
     return pl.pallas_call(
         _gather_kernel,
         grid_spec=pltpu.PrefetchScalarGridSpec(
             num_scalar_prefetch=1,
             grid=(),
             in_specs=[pl.BlockSpec(memory_space=pl.ANY)],
-            out_specs=pl.BlockSpec(memory_space=pltpu.VMEM),
-            scratch_shapes=[pltpu.SemaphoreType.DMA((count,))],
+            out_specs=[
+                pl.BlockSpec(memory_space=pltpu.VMEM),
+                pl.BlockSpec(memory_space=pltpu.VMEM),
+            ],
+            scratch_shapes=[pltpu.SemaphoreType.DMA((count + 1,))],
         ),
-        out_shape=jax.ShapeDtypeStruct((count, rows, width), source.dtype),
-        cost_estimate=pl.CostEstimate(
-            flops=0, transcendentals=0, bytes_accessed=2 * count * rows * width * source.dtype.itemsize
-        ),
+        out_shape=[
+            jax.ShapeDtypeStruct((count, rows, width), source.dtype),
+            jax.ShapeDtypeStruct((tail_rows, width), source.dtype),
+        ],
+        cost_estimate=pl.CostEstimate(flops=0, transcendentals=0, bytes_accessed=2 * moved),
     )(index, source)
 
 
@@ -105,17 +118,12 @@
     ).astype(bf16)
     bc_pieces = lax.all_to_all(bc_part, "dp", split_axis=0, concat_axis=0, tiled=True)
     bc_sum_rows = jnp.sum(bc_pieces.reshape(n_data, bc_rows, width).astype(f32), axis=0)
-    me = lax.axis_index("dp")
-    bc_flat = bc_momentum.reshape(bc_total, width)
-    bc_moment_rows = momentum_decay * lax.dynamic_slice_in_dim(
-        bc_flat, plane * plane_rows + me * bc_rows, bc_rows, axis=0
-    ) + bc_sum_rows
-    bc_copies = jnp.broadcast_to(bc_moment_rows[None], (n_data, bc_rows, width))
-    plane_moment = lax.all_to_all(bc_copies, "dp", split_axis=0, concat_axis=0, tiled=True)
-    plane_moment = plane_moment.reshape(plane_rows, width)
-    plane_copies = jnp.broadcast_to(plane_moment[None], (n_tensor, plane_rows, width))
-    bc_moment = lax.all_to_all(plane_copies, "tensor", split_axis=0, concat_axis=0, tiled=True)
-    bc_moment = bc_moment.reshape(2, STATE, width)
+    bc_copies = jnp.broadcast_to(bc_sum_rows[None], (n_data, bc_rows, width))
+    plane_sum = lax.all_to_all(bc_copies, "dp", split_axis=0, concat_axis=0, tiled=True)
+    plane_sum = plane_sum.reshape(plane_rows, width)
+    plane_copies = jnp.broadcast_to(plane_sum[None], (n_tensor, plane_rows, width))
+    bc_sum = lax.all_to_all(plane_copies, "tensor", split_axis=0, concat_axis=0, tiled=True)
+    bc_moment = momentum_decay * bc_momentum + bc_sum.reshape(2, STATE, width)
     scale = math.sqrt(width)
     bc_update = (orthogonalize(bc_moment) * scale).astype(bf16)
 
@@ -154,8 +162,9 @@
         axis=0,
     )
     everything = lax.all_gather(owned_update, "dp", axis=0, tiled=False)
-    head_update = gather_slabs(everything, head_owner, HD).reshape(heads_here, 3, HD, width)
-    dt_update = lax.dynamic_slice(everything, (dt_owner, HD, 0), (1, heads_here, width))[0]
+    head_update, tail = gather_slabs(everything, owners, HD, chunk - HD)
+    dt_update = tail[:heads_here]
+    head_update = head_update.reshape(heads_here, 3, HD, width)
     return (head_update, dt_update, bc_update, moment[None], bc_moment)
 
 

time: 227 us -> 224 us (0.987)
  blocking collectives: 63.6 us -> 82.9 us
  starting transfers between devices: 9.79 us -> 0.08 us
  waiting for transfers between devices: 72.9 us -> 66.8 us
  local copies, waits for them, and re-layouts: 14.1 us -> 10.3 us
    all_to_all x0 -> x1, blocking collectives: none -> 19 us  [on_device(): lax.all_to_all(bc_part, 'dp', split_axis=0, concat_axis=0, tiled=True)]
    all_to_all x1 -> x0, starting transfers between devices: 9.71 us -> none  [on_device(): lax.all_to_all(bc_part, 'dp', split_axis=0, concat_axis=0, tiled=True)]
    all_to_all x1 -> x0, waiting for transfers between devices: 9.45 us -> none  [on_device(): lax.all_to_all(bc_part, 'dp', split_axis=0, concat_axis=0, tiled=True)]
    unnamed x12 -> x17, local copies, waits for them, and re-layouts: 6.56 us -> 5.04 us
  transfers between devices with their start and end apart: 3 -> 2, of which waited for: 3 -> 2; matrix products, arithmetic and copies ran while one was open for 10% -> 10% of each run, Pallas kernels for 0% -> 0%
where the time goes in v7:
time: 224 us; the launch traced here: 223 us
  blocking collectives  82.9 us (37%)
  waiting for transfers between devices  66.8 us (30%)
  matrix products  32.9 us (15%)
  between operations  15.8 us (7%)
  local copies, waits for them, and re-layouts  10.3 us (5%)
  Pallas kernels  8.59 us (4%)
  other arithmetic  5.89 us (3%)
    all_gather x1, waiting for transfers between devices, on_device(): everything = lax.all_gather(owned_update, 'dp', axis=0, tiled=False)  63.1 us
    all_to_all x1, blocking collectives, on_device(): lax.all_to_all(plane_copies, 'tensor', split_axis=0, concat_axis=0, tiled...  35.2 us
    all_to_all x1, blocking collectives, on_device(): lax.all_to_all(bc_part, 'dp', split_axis=0, concat_axis=0, tiled=True)  19 us
    all_to_all x1, blocking collectives, on_device(): lax.all_to_all(bc_copies, 'dp', split_axis=0, concat_axis=0, tiled=True)  16.3 us
    dot_general x15, matrix products, orthogonalize(): jnp.einsum('bij,bjk->bik', polynomial, current, precision=highest)  12.3 us
    all_gather x1, blocking collectives, on_device(): lax.all_gather(bc_grad, 'tensor', axis=0).astype(f32)  12.3 us
    dot_general x15, matrix products, orthogonalize(): jnp.einsum('bik,bjk->bij', current, current, precision=highest)  10.4 us
    pallas_call x1, Pallas kernels, gather_slabs(): pl.pallas_call(_gather_kernel, grid_spec=pltpu.PrefetchScalarGridSpec(num...  8.59 us
  transfers between devices with their start and end apart: 2, of which 2 were waited for; matrix products, arithmetic and copies ran while one was open for 10% of the time, Pallas kernels for 0%

profile of v7, /device:TPU:1, one launch (start us, length us, event | category | flops | bytes accessed | tf_op | source)
XLA Modules:
  0.0 223.2 jit_solution(17615527859485864696)
XLA Ops:
  7.2 1.2 slice.21
  9.8 1.1 copy.20
  12.0 1.2 copy.19
  15.4 6.6 %convolution_convert_fusion = bf16[2560,2560]{1,0:T(8,128)(2,1)} fusion(bf16[256,2560]{0,1:T(8,128)(2,1)S(1)} %bitcast.114, bf16[128,2560]{1,0:T(8,128)(2,1)S(1)} %copy-done.4, bf16[128,2560]{1,0:T(8,128)(2,1)S(1)} %copy-done), kind=kOutput, calls=%fused_computation | convolution fusion | flops 3364618240 | bytes 15728640 | tf_op jit(solution)/shard_map/dot_general | solution.py:148
  22.9 12.3 %all-gather = bf16[512,256]{1,0:T(8,128)(2,1)S(1)} all-gather(bf16[128,256]{1,0:T(8,128)(2,1)S(1)} %copy-done.5), channel_id=2, replica_groups=mesh['dp'=32,'tensor'=4] {'tensor'}, dimensions={0}, use_global_device_ids=true | all-gather | bytes 327680 | tf_op jit(solution)/shard_map/all_gather | solution.py:105
  35.9 19.0 %all_to_all.19 = bf16[32,2,2560]{2,1,0:T(2,128)(2,1)S(1)} all-to-all(bf16[32,2,2560]{2,1,0:T(2,128)(2,1)S(1)} %all_to_all.12), channel_id=1, replica_groups=mesh['dp'=32,'tensor'=4] {'dp'}, dimensions={0} | all-to-all | bytes 655360 | tf_op jit(solution)/shard_map/all_to_all | solution.py:119
  55.4 16.3 %all_to_all.20 = f32[32,2,2560]{2,1,0:T(2,128)S(1)} all-to-all(f32[32,2,2560]{2,1,0:T(2,128)S(1)} %broadcast_in_dim.13), channel_id=1, replica_groups=mesh['dp'=32,'tensor'=4] {'dp'}, dimensions={0} | all-to-all | bytes 1310720 | tf_op jit(solution)/shard_map/all_to_all | solution.py:122
  72.5 35.2 %all_to_all.21 = f32[4,64,2560]{2,1,0:T(8,128)S(1)} all-to-all(f32[4,64,2560]{2,1,0:T(8,128)S(1)} %broadcast_in_dim.15), channel_id=1, replica_groups=mesh['dp'=32,'tensor'=4] {'tensor'}, dimensions={0} | all-to-all | bytes 5242880 | tf_op jit(solution)/shard_map/all_to_all | solution.py:125
  108.4 1.4 fusion.28
  110.1 1.6 convolution_add_fusion.4
  111.7 1.4 fusion.38
  113.3 1.5 convolution_add_fusion.3
  114.9 1.4 fusion.39
  116.5 1.5 convolution_add_fusion.2
  118.1 1.4 fusion.40
  119.7 1.5 convolution_add_fusion.1
  121.3 1.6 fusion.41
  123.2 2.7 %fusion.1 = bf16[2,128,2560]{2,1,0:T(8,128)(2,1)} fusion(f32[2,128,128]{2,1,0:T(8,128)S(1)} %fusion.10, f32[2,128,2560]{2,1,0:T(8,128)S(1)} %convolution_add_fusion.1), kind=kOutput, calls=%fused_computation.7 | convolution fusion | flops 505937920 | bytes 4063232 | tf_op jit(solution)/shard_map/bij,bjk->bik/dot_general | solution.py:29
  125.8 3.6 %reduce-scatter.2.cloned.1.call-done = bf16[80,2560]{1,0:T(8,128)(2,1)} async-done(((bf16[2560,2560]{1,0:T(8,128)(2,1)}), bf16[80,2560]{1,0:T(8,128)(2,1)}) %reduce-scatter.2.cloned.1.call-update) | async-done | bytes 409616 | tf_op jit(solution)/shard_map/reduce_scatter | solution.py:149
  129.5 1.1 bitcast_add_fusion.1
  141.5 0.9 maximum_maximum_fusion.1
  143.0 1.6 copy.25
  144.6 63.1 %all-gather.4.cloned.1.call-done = bf16[2560,2560]{1,0:T(8,128)(2,1)} async-done(((bf16[80,2560]{1,0:T(8,128)(2,1)}), bf16[2560,2560]{1,0:T(8,128)(2,1)}) %all-gather.4.cloned.1.call-update) | async-done | bytes 13107216 | tf_op jit(solution)/shard_map/all_gather | solution.py:164
  207.8 8.6 %shard_map.128 = (bf16[30,64,2560]{2,1,0:T(8,128)(2,1)}, bf16[16,2560]{1,0:T(8,128)(2,1)}) custom-call(s32[31]{0:T(128)} %clamp_bitcast_fusion.index_ref, bf16[32,80,2560]{2,1,0:T(8,128)(2,1)} %bitcast.111), custom_call_target="tpu_custom_call" | custom-call | bytes 19824640 | tf_op jit(solution)/shard_map/pallas_call | solution.py:61
  (78 shorter events, 19.2 us)
Async XLA Ops:
  7.2 122.3 %reduce-scatter.2.cloned.1.call-start = ((), (), s32[]{:S(2)}) async-start(), calls=%async_computation.4 | async-start | bytes 13516800 | tf_op jit(solution)/shard_map/reduce_scatter | solution.py:149
  14.1 1.1 copy-start
  14.2 1.3 copy-start.4
  22.1 0.8 copy-start.5
  22.1 185.7 %all-gather.4.cloned.1.call-start = ((), (), s32[]{:S(2)}) async-start(), calls=%async_computation.5 | async-start | bytes 13516800 | tf_op jit(solution)/shard_map/all_gather | solution.py:164
  72.5 35.2 %copy-start.1 = (f32[2,128,2560]{2,1,0:T(8,128)S(1)}, f32[2,128,2560]{2,1,0:T(8,128)}, u32[]{:S(2)}) copy-start(f32[2,128,2560]{2,1,0:T(8,128)} %param.17) | copy-start | bytes 7864324
  108.4 1.7 copy-start.2
  122.9 6.5 %copy-start.3 = (f32[1,74,2560]{2,0,1:T(1,128)S(1)}, f32[1,74,2560]{2,0,1:T(1,128)}, u32[]{:S(2)}) copy-start(f32[1,74,2560]{2,0,1:T(1,128)} %param.16) | copy-start | bytes 2273284
  139.9 2.6 %copy-start.6 = (s32[1,31]{1,0:T(1,128)S(1)}, s32[1,31]{1,0:T(1,128)}, u32[]{:S(2)}) copy-start(s32[1,31]{1,0:T(1,128)} %param.15) | copy-start | bytes 376
Sparse Core Ops, SparseCore 0:
  22.2 107.2 reduce-scatter.1
  142.5 65.1 all-gather.3

commit v8 on v7

--- a/solution.py
+++ b/solution.py
@@ -65,8 +65,8 @@
             grid=(),
             in_specs=[pl.BlockSpec(memory_space=pl.ANY)],
             out_specs=[
-                pl.BlockSpec(memory_space=pltpu.VMEM),
-                pl.BlockSpec(memory_space=pltpu.VMEM),
+                pl.BlockSpec(memory_space=pl.ANY),
+                pl.BlockSpec(memory_space=pl.ANY),
             ],
             scratch_shapes=[pltpu.SemaphoreType.DMA((count + 1,))],
         ),

time: 224 us -> 517 us (2.31)
  Pallas kernels: 8.59 us -> 302 us
    pallas_call x1, Pallas kernels: 8.59 us -> 302 us  [gather_slabs(): pl.pallas_call(_gather_kernel, grid_spec=pltpu.PrefetchScalarGridSpec(num...]
  transfers between devices with their start and end apart: 2 -> 2, of which waited for: 2 -> 2; matrix products, arithmetic and copies ran while one was open for 10% -> 4% of each run, Pallas kernels for 0% -> 0%
where the time goes in v8:
time: 517 us
  Pallas kernels  302 us (58%)
  blocking collectives  82.9 us (16%)
  waiting for transfers between devices  66.8 us (13%)
  matrix products  32.9 us (6%)
  between operations  15.8 us (3%)
  local copies, waits for them, and re-layouts  10.3 us (2%)
  other arithmetic  5.89 us (1%)
    pallas_call x1, Pallas kernels, gather_slabs(): pl.pallas_call(_gather_kernel, grid_spec=pltpu.PrefetchScalarGridSpec(num...  302 us
    all_gather x1, waiting for transfers between devices, on_device(): everything = lax.all_gather(owned_update, 'dp', axis=0, tiled=False)  63.1 us
    all_to_all x1, blocking collectives, on_device(): lax.all_to_all(plane_copies, 'tensor', split_axis=0, concat_axis=0, tiled...  35.2 us
    all_to_all x1, blocking collectives, on_device(): lax.all_to_all(bc_part, 'dp', split_axis=0, concat_axis=0, tiled=True)  19 us
    all_to_all x1, blocking collectives, on_device(): lax.all_to_all(bc_copies, 'dp', split_axis=0, concat_axis=0, tiled=True)  16.3 us
    dot_general x15, matrix products, orthogonalize(): jnp.einsum('bij,bjk->bik', polynomial, current, precision=highest)  12.3 us
    all_gather x1, blocking collectives, on_device(): lax.all_gather(bc_grad, 'tensor', axis=0).astype(f32)  12.3 us
    dot_general x15, matrix products, orthogonalize(): jnp.einsum('bik,bjk->bij', current, current, precision=highest)  10.4 us
  transfers between devices with their start and end apart: 2, of which 2 were waited for; matrix products, arithmetic and copies ran while one was open for 4% of the time, Pallas kernels for 0%

profile of v8, /device:TPU:1, one launch (start us, length us, event | category | flops | bytes accessed | tf_op | source)
XLA Modules:
  0.0 517.0 jit_solution(10673355145757278606)
XLA Ops:
  7.2 1.2 slice.21
  9.8 1.1 copy.20
  12.0 1.2 copy.19
  15.4 6.6 %convolution_convert_fusion = bf16[2560,2560]{1,0:T(8,128)(2,1)} fusion(bf16[256,2560]{0,1:T(8,128)(2,1)S(1)} %bitcast.114, bf16[128,2560]{1,0:T(8,128)(2,1)S(1)} %copy-done.4, bf16[128,2560]{1,0:T(8,128)(2,1)S(1)} %copy-done), kind=kOutput, calls=%fused_computation | convolution fusion | flops 3364618240 | bytes 15728640 | tf_op jit(solution)/shard_map/dot_general | solution.py:148
  22.9 12.3 %all-gather = bf16[512,256]{1,0:T(8,128)(2,1)S(1)} all-gather(bf16[128,256]{1,0:T(8,128)(2,1)S(1)} %copy-done.5), channel_id=2, replica_groups=mesh['dp'=32,'tensor'=4] {'tensor'}, dimensions={0}, use_global_device_ids=true | all-gather | bytes 327680 | tf_op jit(solution)/shard_map/all_gather | solution.py:105
  35.9 19.0 %all_to_all.19 = bf16[32,2,2560]{2,1,0:T(2,128)(2,1)S(1)} all-to-all(bf16[32,2,2560]{2,1,0:T(2,128)(2,1)S(1)} %all_to_all.12), channel_id=1, replica_groups=mesh['dp'=32,'tensor'=4] {'dp'}, dimensions={0} | all-to-all | bytes 655360 | tf_op jit(solution)/shard_map/all_to_all | solution.py:119
  55.4 16.3 %all_to_all.20 = f32[32,2,2560]{2,1,0:T(2,128)S(1)} all-to-all(f32[32,2,2560]{2,1,0:T(2,128)S(1)} %broadcast_in_dim.13), channel_id=1, replica_groups=mesh['dp'=32,'tensor'=4] {'dp'}, dimensions={0} | all-to-all | bytes 1310720 | tf_op jit(solution)/shard_map/all_to_all | solution.py:122
  72.5 35.2 %all_to_all.21 = f32[4,64,2560]{2,1,0:T(8,128)S(1)} all-to-all(f32[4,64,2560]{2,1,0:T(8,128)S(1)} %broadcast_in_dim.15), channel_id=1, replica_groups=mesh['dp'=32,'tensor'=4] {'tensor'}, dimensions={0} | all-to-all | bytes 5242880 | tf_op jit(solution)/shard_map/all_to_all | solution.py:125
  108.4 1.4 fusion.28
  110.1 1.6 convolution_add_fusion.4
  111.7 1.4 fusion.38
  113.3 1.5 convolution_add_fusion.3
  114.9 1.4 fusion.39
  116.5 1.5 convolution_add_fusion.2
  118.1 1.4 fusion.40
  119.7 1.5 convolution_add_fusion.1
  121.3 1.6 fusion.41
  123.2 2.7 fusion.1
  125.8 3.6 reduce-scatter.2.cloned.1.call-done
  129.5 1.1 bitcast_add_fusion.1
  141.5 0.9 maximum_maximum_fusion.1
  143.0 1.6 copy.25
  144.6 63.1 %all-gather.4.cloned.1.call-done = bf16[2560,2560]{1,0:T(8,128)(2,1)} async-done(((bf16[80,2560]{1,0:T(8,128)(2,1)}), bf16[2560,2560]{1,0:T(8,128)(2,1)}) %all-gather.4.cloned.1.call-update) | async-done | bytes 13107216 | tf_op jit(solution)/shard_map/all_gather | solution.py:164
  207.8 302.3 %shard_map.128 = (bf16[30,64,2560]{2,1,0:T(8,128)(2,1)}, bf16[16,2560]{1,0:T(8,128)(2,1)}) custom-call(s32[31]{0:T(128)} %clamp_bitcast_fusion.index_ref, bf16[32,80,2560]{2,1,0:T(8,128)(2,1)} %bitcast.111), custom_call_target="tpu_custom_call" | custom-call | bytes 19824640 | tf_op jit(solution)/shard_map/pallas_call | solution.py:61
  (78 shorter events, 19.2 us)
Async XLA Ops:
  7.2 122.3 %reduce-scatter.2.cloned.1.call-start = ((), (), s32[]{:S(2)}) async-start(), calls=%async_computation.4 | async-start | bytes 13516800 | tf_op jit(solution)/shard_map/reduce_scatter | solution.py:149
  14.1 1.1 copy-start
  14.2 1.3 copy-start.4
  22.1 0.8 copy-start.5
  22.1 185.7 %all-gather.4.cloned.1.call-start = ((), (), s32[]{:S(2)}) async-start(), calls=%async_computation.5 | async-start | bytes 13516800 | tf_op jit(solution)/shard_map/all_gather | solution.py:164
  72.5 35.2 %copy-start.1 = (f32[2,128,2560]{2,1,0:T(8,128)S(1)}, f32[2,128,2560]{2,1,0:T(8,128)}, u32[]{:S(2)}) copy-start(f32[2,128,2560]{2,1,0:T(8,128)} %param.17) | copy-start | bytes 7864324
  108.4 1.7 copy-start.2
  122.9 6.5 %copy-start.3 = (f32[1,74,2560]{2,0,1:T(1,128)S(1)}, f32[1,74,2560]{2,0,1:T(1,128)}, u32[]{:S(2)}) copy-start(f32[1,74,2560]{2,0,1:T(1,128)} %param.16) | copy-start | bytes 2273284
  139.9 2.6 copy-start.6
Sparse Core Ops, SparseCore 0:
  22.2 107.2 reduce-scatter.1
  142.5 65.1 all-gather.3

commit v9 on v7

--- a/solution.py
+++ b/solution.py
@@ -151,8 +151,12 @@
     owned_sum = owned[:capacity].astype(f32)
 
     moment = momentum_decay * head_momentum[0] + owned_sum
-    head_direction = orthogonalize(moment[None, :HD])[0]
-    dt_direction = orthogonalize(moment[None, HD:])[0]
+    dt_padded = jnp.concatenate(
+        [moment[HD:], jnp.zeros((2 * HD - capacity, width), f32)], axis=0
+    )
+    directions = orthogonalize(jnp.stack([moment[:HD], dt_padded]))
+    head_direction = directions[0]
+    dt_direction = directions[1, : capacity - HD]
     owned_update = jnp.concatenate(
         [
             (head_direction * scale).astype(bf16),

time: 224 us -> 221 us (0.987)
    unnamed x17 -> x19, local copies, waits for them, and re-layouts: 5.04 us -> 4.26 us
    dot_general x15 -> x10, matrix products: 10.4 us -> 11 us  [orthogonalize(): jnp.einsum('bik,bjk->bij', current, current, precision=highest)]
    dot_general x15 -> x10, matrix products: 12.3 us -> 12.9 us  [orthogonalize(): jnp.einsum('bij,bjk->bik', polynomial, current, precision=highest)]
where the time goes in v9:
time: 221 us
  blocking collectives  82.9 us (38%)
  waiting for transfers between devices  66.8 us (30%)
  matrix products  33.4 us (15%)
  between operations  14.5 us (7%)
  local copies, waits for them, and re-layouts  9.64 us (4%)
  Pallas kernels  8.59 us (4%)
  other arithmetic  4.85 us (2%)
    all_gather x1, waiting for transfers between devices, on_device(): everything = lax.all_gather(owned_update, 'dp', axis=0, tiled=False)  63.1 us
    all_to_all x1, blocking collectives, on_device(): lax.all_to_all(plane_copies, 'tensor', split_axis=0, concat_axis=0, tiled...  35.2 us
    all_to_all x1, blocking collectives, on_device(): lax.all_to_all(bc_part, 'dp', split_axis=0, concat_axis=0, tiled=True)  19 us
    all_to_all x1, blocking collectives, on_device(): lax.all_to_all(bc_copies, 'dp', split_axis=0, concat_axis=0, tiled=True)  16.3 us
    dot_general x10, matrix products, orthogonalize(): jnp.einsum('bij,bjk->bik', polynomial, current, precision=highest)  12.9 us
    all_gather x1, blocking collectives, on_device(): lax.all_gather(bc_grad, 'tensor', axis=0).astype(f32)  12.3 us
    dot_general x10, matrix products, orthogonalize(): jnp.einsum('bik,bjk->bij', current, current, precision=highest)  11 us
    pallas_call x1, Pallas kernels, gather_slabs(): pl.pallas_call(_gather_kernel, grid_spec=pltpu.PrefetchScalarGridSpec(num...  8.59 us
  transfers between devices with their start and end apart: 2, of which 2 were waited for; matrix products, arithmetic and copies ran while one was open for 10% of the time, Pallas kernels for 0%

profile of v9, /device:TPU:1, one launch (start us, length us, event | category | flops | bytes accessed | tf_op | source)
XLA Modules:
  0.0 220.8 jit_solution(16398712882800427306)
XLA Ops:
  7.2 1.3 slice.27
  9.8 1.1 copy.20
  14.7 6.7 %convolution_convert_fusion = bf16[2560,2560]{1,0:T(8,128)(2,1)} fusion(bf16[256,2560]{0,1:T(8,128)(2,1)S(1)} %bitcast.95, bf16[128,2560]{1,0:T(8,128)(2,1)S(1)} %copy-done.4, bf16[128,2560]{1,0:T(8,128)(2,1)S(1)} %copy-done), kind=kOutput, calls=%fused_computation | convolution fusion | flops 3364618240 | bytes 15728640 | tf_op jit(solution)/shard_map/dot_general | solution.py:148
  22.2 12.3 %all-gather = bf16[512,256]{1,0:T(8,128)(2,1)S(1)} all-gather(bf16[128,256]{1,0:T(8,128)(2,1)S(1)} %copy-done.6), channel_id=2, replica_groups=mesh['dp'=32,'tensor'=4] {'tensor'}, dimensions={0}, use_global_device_ids=true | all-gather | bytes 327680 | tf_op jit(solution)/shard_map/all_gather | solution.py:105
  35.2 19.0 %all_to_all.19 = bf16[32,2,2560]{2,1,0:T(2,128)(2,1)S(1)} all-to-all(bf16[32,2,2560]{2,1,0:T(2,128)(2,1)S(1)} %all_to_all.12), channel_id=1, replica_groups=mesh['dp'=32,'tensor'=4] {'dp'}, dimensions={0} | all-to-all | bytes 655360 | tf_op jit(solution)/shard_map/all_to_all | solution.py:119
  54.7 16.3 %all_to_all.20 = f32[32,2,2560]{2,1,0:T(2,128)S(1)} all-to-all(f32[32,2,2560]{2,1,0:T(2,128)S(1)} %broadcast_in_dim.13), channel_id=1, replica_groups=mesh['dp'=32,'tensor'=4] {'dp'}, dimensions={0} | all-to-all | bytes 1310720 | tf_op jit(solution)/shard_map/all_to_all | solution.py:122
  71.8 35.2 %all_to_all.21 = f32[4,64,2560]{2,1,0:T(8,128)S(1)} all-to-all(f32[4,64,2560]{2,1,0:T(8,128)S(1)} %broadcast_in_dim.15), channel_id=1, replica_groups=mesh['dp'=32,'tensor'=4] {'tensor'}, dimensions={0} | all-to-all | bytes 5242880 | tf_op jit(solution)/shard_map/all_to_all | solution.py:125
  107.8 1.4 fusion.21
  109.4 1.6 convolution_add_fusion.4
  111.0 1.4 fusion.35
  112.7 1.5 convolution_add_fusion.3
  114.2 1.4 fusion.36
  115.9 1.5 convolution_add_fusion.2
  117.4 1.4 fusion.37
  119.0 1.5 convolution_add_fusion.1
  120.6 1.6 fusion.38
  122.5 2.7 %fusion.1 = bf16[2,128,2560]{2,1,0:T(8,128)(2,1)} fusion(f32[2,128,128]{2,1,0:T(8,128)S(1)} %fusion.6, f32[2,128,2560]{2,1,0:T(8,128)S(1)} %convolution_add_fusion.1), kind=kOutput, calls=%fused_computation.7 | convolution fusion | flops 505937920 | bytes 4063232 | tf_op jit(solution)/shard_map/bij,bjk->bik/dot_general | solution.py:29
  125.2 3.6 %reduce-scatter.2.cloned.1.call-done = bf16[80,2560]{1,0:T(8,128)(2,1)} async-done(((bf16[2560,2560]{1,0:T(8,128)(2,1)}), bf16[80,2560]{1,0:T(8,128)(2,1)}) %reduce-scatter.2.cloned.1.call-update) | async-done | bytes 409616 | tf_op jit(solution)/shard_map/reduce_scatter | solution.py:149
  128.8 1.1 bitcast_add_fusion.1
  131.3 0.9 convolution_add_fusion.9
  139.1 0.9 maximum_maximum_fusion.1
  140.5 1.6 copy.25
  142.2 63.1 %all-gather.4.cloned.1.call-done = bf16[2560,2560]{1,0:T(8,128)(2,1)} async-done(((bf16[80,2560]{1,0:T(8,128)(2,1)}), bf16[2560,2560]{1,0:T(8,128)(2,1)}) %all-gather.4.cloned.1.call-update) | async-done | bytes 13107216 | tf_op jit(solution)/shard_map/all_gather | solution.py:168
  205.3 8.6 %shard_map.128 = (bf16[30,64,2560]{2,1,0:T(8,128)(2,1)}, bf16[16,2560]{1,0:T(8,128)(2,1)}) custom-call(s32[31]{0:T(128)} %clamp_bitcast_fusion.index_ref, bf16[32,80,2560]{2,1,0:T(8,128)(2,1)} %bitcast.92), custom_call_target="tpu_custom_call" | custom-call | bytes 19824640 | tf_op jit(solution)/shard_map/pallas_call | solution.py:61
  (69 shorter events, 18.2 us)
Async XLA Ops:
  7.2 4.8 %copy-start.5 = (bf16[128,1280]{1,0:T(8,128)(2,1)S(1)}, bf16[128,1280]{1,0:T(8,128)(2,1)}, u32[]{:S(2)}) copy-start(bf16[128,1280]{1,0:T(8,128)(2,1)} %param.12) | copy-start | bytes 983044
  7.2 121.6 %reduce-scatter.2.cloned.1.call-start = ((), (), s32[]{:S(2)}) async-start(), calls=%async_computation.4 | async-start | bytes 13516800 | tf_op jit(solution)/shard_map/reduce_scatter | solution.py:149
  13.4 1.1 copy-start
  13.4 1.3 copy-start.4
  21.4 0.8 copy-start.6
  21.4 183.9 %all-gather.4.cloned.1.call-start = ((), (), s32[]{:S(2)}) async-start(), calls=%async_computation.5 | async-start | bytes 13516800 | tf_op jit(solution)/shard_map/all_gather | solution.py:168
  71.8 35.2 %copy-start.1 = (f32[2,128,2560]{2,1,0:T(8,128)S(1)}, f32[2,128,2560]{2,1,0:T(8,128)}, u32[]{:S(2)}) copy-start(f32[2,128,2560]{2,1,0:T(8,128)} %param.17) | copy-start | bytes 7864324
  107.7 1.7 copy-start.2
  122.5 6.3 %copy-start.3 = (f32[1,74,2560]{2,0,1:T(1,128)S(1)}, f32[1,74,2560]{2,0,1:T(1,128)}, u32[]{:S(2)}) copy-start(f32[1,74,2560]{2,0,1:T(1,128)} %param.16) | copy-start | bytes 2273284
  139.0 1.0 copy-start.7
Sparse Core Ops, SparseCore 0:
  21.5 107.2 reduce-scatter.1
  140.1 65.1 all-gather.3

commit v10 on v9

--- a/solution.py
+++ b/solution.py
@@ -32,24 +32,30 @@
     return current
 
 
-def _gather_kernel(index_ref, source_ref, out_ref, tail_ref, sems):
-    count, rows = out_ref.shape[0], out_ref.shape[1]
-    tail_rows = tail_ref.shape[0]
-    copies = []
-    for b in range(count):
-        copies.append(
-            pltpu.make_async_copy(
-                source_ref.at[index_ref[b], pl.ds(0, rows)], out_ref.at[b], sems.at[b]
-            )
-        )
-    copies.append(
+def _gather_kernel(index_ref, source_ref, out_ref, tail_ref, slabs, tail_slab, in_sems, out_sems):
+    count, rows = slabs.shape[0], slabs.shape[1]
+    tail_rows = tail_slab.shape[0]
+    inbound = [
         pltpu.make_async_copy(
-            source_ref.at[index_ref[count], pl.ds(rows, tail_rows)], tail_ref, sems.at[count]
-        )
-    )
-    for copy in copies:
+            source_ref.at[index_ref[b], pl.ds(0, rows)], slabs.at[b], in_sems.at[b]
+        )
+        for b in range(count)
+    ]
+    inbound.append(
+        pltpu.make_async_copy(
+            source_ref.at[index_ref[count], pl.ds(rows, tail_rows)], tail_slab, in_sems.at[count]
+        )
+    )
+    outbound = [
+        pltpu.make_async_copy(slabs.at[b], out_ref.at[b], out_sems.at[b]) for b in range(count)
+    ]
+    outbound.append(pltpu.make_async_copy(tail_slab, tail_ref, out_sems.at[count]))
+    for copy in inbound:
         copy.start()
-    for copy in copies:
+    for copy_in, copy_out in zip(inbound, outbound):
+        copy_in.wait()
+        copy_out.start()
+    for copy in outbound:
         copy.wait()
 
 
@@ -65,10 +71,15 @@
             grid=(),
             in_specs=[pl.BlockSpec(memory_space=pl.ANY)],
             out_specs=[
-                pl.BlockSpec(memory_space=pltpu.VMEM),
-                pl.BlockSpec(memory_space=pltpu.VMEM),
+                pl.BlockSpec(memory_space=pl.ANY),
+                pl.BlockSpec(memory_space=pl.ANY),
             ],
-            scratch_shapes=[pltpu.SemaphoreType.DMA((count + 1,))],
+            scratch_shapes=[
+                pltpu.VMEM((count, rows, width), source.dtype),
+                pltpu.VMEM((tail_rows, width), source.dtype),
+                pltpu.SemaphoreType.DMA((count + 1,)),
+                pltpu.SemaphoreType.DMA((count + 1,)),
+            ],
         ),
         out_shape=[
             jax.ShapeDtypeStruct((count, rows, width), source.dtype),

time: 221 us -> 221 us (level)
  no operation moved by 1% of the time
where the time goes in v10:
time: 221 us
  blocking collectives  82.9 us (38%)
  waiting for transfers between devices  66.8 us (30%)
  matrix products  33.4 us (15%)
  between operations  14.5 us (7%)
  local copies, waits for them, and re-layouts  9.64 us (4%)
  Pallas kernels  8.57 us (4%)
  other arithmetic  4.85 us (2%)
    all_gather x1, waiting for transfers between devices, on_device(): everything = lax.all_gather(owned_update, 'dp', axis=0, tiled=False)  63.1 us
    all_to_all x1, blocking collectives, on_device(): lax.all_to_all(plane_copies, 'tensor', split_axis=0, concat_axis=0, tiled...  35.2 us
    all_to_all x1, blocking collectives, on_device(): lax.all_to_all(bc_part, 'dp', split_axis=0, concat_axis=0, tiled=True)  19 us
    all_to_all x1, blocking collectives, on_device(): lax.all_to_all(bc_copies, 'dp', split_axis=0, concat_axis=0, tiled=True)  16.3 us
    dot_general x10, matrix products, orthogonalize(): jnp.einsum('bij,bjk->bik', polynomial, current, precision=highest)  12.9 us
    all_gather x1, blocking collectives, on_device(): lax.all_gather(bc_grad, 'tensor', axis=0).astype(f32)  12.3 us
    dot_general x10, matrix products, orthogonalize(): jnp.einsum('bik,bjk->bij', current, current, precision=highest)  11 us
    pallas_call x1, Pallas kernels, gather_slabs(): pl.pallas_call(_gather_kernel, grid_spec=pltpu.PrefetchScalarGridSpec(num...  8.57 us
  transfers between devices with their start and end apart: 2, of which 2 were waited for; matrix products, arithmetic and copies ran while one was open for 10% of the time, Pallas kernels for 0%

profile of v10, /device:TPU:1, one launch (start us, length us, event | category | flops | bytes accessed | tf_op | source)
XLA Modules:
  0.0 220.7 jit_solution(9678312452427558927)
XLA Ops:
  7.2 1.3 slice.27
  9.8 1.1 copy.20
  14.7 6.7 %convolution_convert_fusion = bf16[2560,2560]{1,0:T(8,128)(2,1)} fusion(bf16[256,2560]{0,1:T(8,128)(2,1)S(1)} %bitcast.95, bf16[128,2560]{1,0:T(8,128)(2,1)S(1)} %copy-done.4, bf16[128,2560]{1,0:T(8,128)(2,1)S(1)} %copy-done), kind=kOutput, calls=%fused_computation | convolution fusion | flops 3364618240 | bytes 15728640 | tf_op jit(solution)/shard_map/dot_general | solution.py:159
  22.2 12.3 %all-gather = bf16[512,256]{1,0:T(8,128)(2,1)S(1)} all-gather(bf16[128,256]{1,0:T(8,128)(2,1)S(1)} %copy-done.6), channel_id=2, replica_groups=mesh['dp'=32,'tensor'=4] {'tensor'}, dimensions={0}, use_global_device_ids=true | all-gather | bytes 327680 | tf_op jit(solution)/shard_map/all_gather | solution.py:116
  35.2 19.0 %all_to_all.19 = bf16[32,2,2560]{2,1,0:T(2,128)(2,1)S(1)} all-to-all(bf16[32,2,2560]{2,1,0:T(2,128)(2,1)S(1)} %all_to_all.12), channel_id=1, replica_groups=mesh['dp'=32,'tensor'=4] {'dp'}, dimensions={0} | all-to-all | bytes 655360 | tf_op jit(solution)/shard_map/all_to_all | solution.py:130
  54.7 16.3 %all_to_all.20 = f32[32,2,2560]{2,1,0:T(2,128)S(1)} all-to-all(f32[32,2,2560]{2,1,0:T(2,128)S(1)} %broadcast_in_dim.13), channel_id=1, replica_groups=mesh['dp'=32,'tensor'=4] {'dp'}, dimensions={0} | all-to-all | bytes 1310720 | tf_op jit(solution)/shard_map/all_to_all | solution.py:133
  71.8 35.2 %all_to_all.21 = f32[4,64,2560]{2,1,0:T(8,128)S(1)} all-to-all(f32[4,64,2560]{2,1,0:T(8,128)S(1)} %broadcast_in_dim.15), channel_id=1, replica_groups=mesh['dp'=32,'tensor'=4] {'tensor'}, dimensions={0} | all-to-all | bytes 5242880 | tf_op jit(solution)/shard_map/all_to_all | solution.py:136
  107.8 1.4 fusion.21
  109.4 1.6 convolution_add_fusion.4
  111.0 1.4 fusion.35
  112.7 1.5 convolution_add_fusion.3
  114.2 1.4 fusion.36
  115.9 1.5 convolution_add_fusion.2
  117.4 1.4 fusion.37
  119.0 1.5 convolution_add_fusion.1
  120.6 1.6 fusion.38
  122.5 2.7 %fusion.1 = bf16[2,128,2560]{2,1,0:T(8,128)(2,1)} fusion(f32[2,128,128]{2,1,0:T(8,128)S(1)} %fusion.6, f32[2,128,2560]{2,1,0:T(8,128)S(1)} %convolution_add_fusion.1), kind=kOutput, calls=%fused_computation.7 | convolution fusion | flops 505937920 | bytes 4063232 | tf_op jit(solution)/shard_map/bij,bjk->bik/dot_general | solution.py:29
  125.2 3.6 %reduce-scatter.2.cloned.1.call-done = bf16[80,2560]{1,0:T(8,128)(2,1)} async-done(((bf16[2560,2560]{1,0:T(8,128)(2,1)}), bf16[80,2560]{1,0:T(8,128)(2,1)}) %reduce-scatter.2.cloned.1.call-update) | async-done | bytes 409616 | tf_op jit(solution)/shard_map/reduce_scatter | solution.py:160
  128.8 1.1 bitcast_add_fusion.1
  131.3 0.9 convolution_add_fusion.9
  139.1 0.9 maximum_maximum_fusion.1
  140.5 1.6 copy.25
  142.2 63.1 %all-gather.4.cloned.1.call-done = bf16[2560,2560]{1,0:T(8,128)(2,1)} async-done(((bf16[80,2560]{1,0:T(8,128)(2,1)}), bf16[2560,2560]{1,0:T(8,128)(2,1)}) %all-gather.4.cloned.1.call-update) | async-done | bytes 13107216 | tf_op jit(solution)/shard_map/all_gather | solution.py:179
  205.3 8.6 %shard_map.128 = (bf16[30,64,2560]{2,1,0:T(8,128)(2,1)}, bf16[16,2560]{1,0:T(8,128)(2,1)}) custom-call(s32[31]{0:T(128)} %clamp_bitcast_fusion.index_ref, bf16[32,80,2560]{2,1,0:T(8,128)(2,1)} %bitcast.92), custom_call_target="tpu_custom_call" | custom-call | bytes 19824640 | tf_op jit(solution)/shard_map/pallas_call | solution.py:67
  (69 shorter events, 18.2 us)
Async XLA Ops:
  7.2 4.8 %copy-start.5 = (bf16[128,1280]{1,0:T(8,128)(2,1)S(1)}, bf16[128,1280]{1,0:T(8,128)(2,1)}, u32[]{:S(2)}) copy-start(bf16[128,1280]{1,0:T(8,128)(2,1)} %param.12) | copy-start | bytes 983044
  7.2 121.6 %reduce-scatter.2.cloned.1.call-start = ((), (), s32[]{:S(2)}) async-start(), calls=%async_computation.4 | async-start | bytes 13516800 | tf_op jit(solution)/shard_map/reduce_scatter | solution.py:160
  13.4 1.1 copy-start
  13.4 1.3 copy-start.4
  21.4 0.8 copy-start.6
  21.4 183.9 %all-gather.4.cloned.1.call-start = ((), (), s32[]{:S(2)}) async-start(), calls=%async_computation.5 | async-start | bytes 13516800 | tf_op jit(solution)/shard_map/all_gather | solution.py:179
  71.8 35.2 %copy-start.1 = (f32[2,128,2560]{2,1,0:T(8,128)S(1)}, f32[2,128,2560]{2,1,0:T(8,128)}, u32[]{:S(2)}) copy-start(f32[2,128,2560]{2,1,0:T(8,128)} %param.17) | copy-start | bytes 7864324
  107.7 1.7 copy-start.2
  122.5 6.3 %copy-start.3 = (f32[1,74,2560]{2,0,1:T(1,128)S(1)}, f32[1,74,2560]{2,0,1:T(1,128)}, u32[]{:S(2)}) copy-start(f32[1,74,2560]{2,0,1:T(1,128)} %param.16) | copy-start | bytes 2273284
  139.0 1.0 copy-start.7
Sparse Core Ops, SparseCore 0:
  21.5 107.2 reduce-scatter.1
  140.1 65.1 all-gather.3

commit v11 on v9

--- a/solution.py
+++ b/solution.py
@@ -118,12 +118,12 @@
     ).astype(bf16)
     bc_pieces = lax.all_to_all(bc_part, "dp", split_axis=0, concat_axis=0, tiled=True)
     bc_sum_rows = jnp.sum(bc_pieces.reshape(n_data, bc_rows, width).astype(f32), axis=0)
-    bc_copies = jnp.broadcast_to(bc_sum_rows[None], (n_data, bc_rows, width))
+    bc_copies = jnp.broadcast_to(bc_sum_rows.astype(bf16)[None], (n_data, bc_rows, width))
     plane_sum = lax.all_to_all(bc_copies, "dp", split_axis=0, concat_axis=0, tiled=True)
     plane_sum = plane_sum.reshape(plane_rows, width)
     plane_copies = jnp.broadcast_to(plane_sum[None], (n_tensor, plane_rows, width))
     bc_sum = lax.all_to_all(plane_copies, "tensor", split_axis=0, concat_axis=0, tiled=True)
-    bc_moment = momentum_decay * bc_momentum + bc_sum.reshape(2, STATE, width)
+    bc_moment = momentum_decay * bc_momentum + bc_sum.astype(f32).reshape(2, STATE, width)
     scale = math.sqrt(width)
     bc_update = (orthogonalize(bc_moment) * scale).astype(bf16)
 

time: 221 us -> 221 us (level)
  waiting for transfers between devices: 66.8 us -> 84 us
  blocking collectives: 82.9 us -> 66.1 us
    reduce_scatter x1, waiting for transfers between devices: 3.64 us -> 20.8 us  [on_device(): owned = lax.psum_scatter(send, 'dp', scatter_dimension=0, tiled=True)]
    all_to_all x1, blocking collectives: 35.2 us -> 21.7 us  [on_device(): lax.all_to_all(plane_copies, 'tensor', split_axis=0, concat_axis=0, tiled...]
    all_to_all x1, blocking collectives: 16.3 us -> 13 us  [on_device(): lax.all_to_all(bc_copies, 'dp', split_axis=0, concat_axis=0, tiled=True)]
where the time goes in v11:
time: 221 us
  waiting for transfers between devices  84 us (38%)
  blocking collectives  66.1 us (30%)
  matrix products  33.4 us (15%)
  between operations  14.5 us (7%)
  local copies, waits for them, and re-layouts  9.12 us (4%)
  Pallas kernels  8.59 us (4%)
  other arithmetic  4.95 us (2%)
    all_gather x1, waiting for transfers between devices, on_device(): everything = lax.all_gather(owned_update, 'dp', axis=0, tiled=False)  63.1 us
    all_to_all x1, blocking collectives, on_device(): lax.all_to_all(plane_copies, 'tensor', split_axis=0, concat_axis=0, tiled...  21.7 us
    reduce_scatter x1, waiting for transfers between devices, on_device(): owned = lax.psum_scatter(send, 'dp', scatter_dimension=0, tiled=True)  20.8 us
    all_to_all x1, blocking collectives, on_device(): lax.all_to_all(bc_part, 'dp', split_axis=0, concat_axis=0, tiled=True)  19 us
    all_to_all x1, blocking collectives, on_device(): lax.all_to_all(bc_copies, 'dp', split_axis=0, concat_axis=0, tiled=True)  13 us
    dot_general x10, matrix products, orthogonalize(): jnp.einsum('bij,bjk->bik', polynomial, current, precision=highest)  12.9 us
    all_gather x1, blocking collectives, on_device(): lax.all_gather(bc_grad, 'tensor', axis=0).astype(f32)  12.3 us
    dot_general x10, matrix products, orthogonalize(): jnp.einsum('bik,bjk->bij', current, current, precision=highest)  11 us
  transfers between devices with their start and end apart: 2, of which 2 were waited for; matrix products, arithmetic and copies ran while one was open for 10% of the time, Pallas kernels for 0%

profile of v11, /device:TPU:1, one launch (start us, length us, event | category | flops | bytes accessed | tf_op | source)
XLA Modules:
  0.0 220.8 jit_solution(1855152875672706358)
XLA Ops:
  7.2 1.3 slice.27
  9.8 1.1 copy.20
  14.7 6.7 %convolution_convert_fusion = bf16[2560,2560]{1,0:T(8,128)(2,1)} fusion(bf16[256,2560]{0,1:T(8,128)(2,1)S(1)} %bitcast.95, bf16[128,2560]{1,0:T(8,128)(2,1)S(1)} %copy-done.4, bf16[128,2560]{1,0:T(8,128)(2,1)S(1)} %copy-done), kind=kOutput, calls=%fused_computation | convolution fusion | flops 3364618240 | bytes 15728640 | tf_op jit(solution)/shard_map/dot_general | solution.py:148
  22.2 12.3 %all-gather = bf16[512,256]{1,0:T(8,128)(2,1)S(1)} all-gather(bf16[128,256]{1,0:T(8,128)(2,1)S(1)} %copy-done.6), channel_id=2, replica_groups=mesh['dp'=32,'tensor'=4] {'tensor'}, dimensions={0}, use_global_device_ids=true | all-gather | bytes 327680 | tf_op jit(solution)/shard_map/all_gather | solution.py:105
  35.2 19.0 %all_to_all.19 = bf16[32,2,2560]{2,1,0:T(2,128)(2,1)S(1)} all-to-all(bf16[32,2,2560]{2,1,0:T(2,128)(2,1)S(1)} %all_to_all.12), channel_id=1, replica_groups=mesh['dp'=32,'tensor'=4] {'dp'}, dimensions={0} | all-to-all | bytes 655360 | tf_op jit(solution)/shard_map/all_to_all | solution.py:119
  54.7 13.0 %all_to_all.20 = bf16[32,2,2560]{2,1,0:T(2,128)(2,1)S(1)} all-to-all(bf16[32,2,2560]{2,1,0:T(2,128)(2,1)S(1)} %broadcast_in_dim.13), channel_id=1, replica_groups=mesh['dp'=32,'tensor'=4] {'dp'}, dimensions={0} | all-to-all | bytes 655360 | tf_op jit(solution)/shard_map/all_to_all | solution.py:122
  68.0 21.7 %all_to_all.21 = bf16[4,64,2560]{2,1,0:T(8,128)(2,1)S(1)} all-to-all(bf16[4,64,2560]{2,1,0:T(8,128)(2,1)S(1)} %broadcast_in_dim.15), channel_id=1, replica_groups=mesh['dp'=32,'tensor'=4] {'tensor'}, dimensions={0} | all-to-all | bytes 2621440 | tf_op jit(solution)/shard_map/all_to_all | solution.py:125
  90.6 1.4 fusion.21
  92.2 1.6 convolution_add_fusion.4
  93.8 1.4 fusion.35
  95.4 1.5 convolution_add_fusion.3
  97.0 1.4 fusion.36
  98.6 1.5 convolution_add_fusion.2
  100.2 1.4 fusion.37
  101.8 1.5 convolution_add_fusion.1
  103.4 1.6 fusion.38
  105.3 2.7 %fusion.1 = bf16[2,128,2560]{2,1,0:T(8,128)(2,1)} fusion(f32[2,128,128]{2,1,0:T(8,128)S(1)} %fusion.6, f32[2,128,2560]{2,1,0:T(8,128)S(1)} %convolution_add_fusion.1), kind=kOutput, calls=%fused_computation.7 | convolution fusion | flops 505937920 | bytes 4063232 | tf_op jit(solution)/shard_map/bij,bjk->bik/dot_general | solution.py:29
  108.0 20.8 %reduce-scatter.2.cloned.1.call-done = bf16[80,2560]{1,0:T(8,128)(2,1)} async-done(((bf16[2560,2560]{1,0:T(8,128)(2,1)}), bf16[80,2560]{1,0:T(8,128)(2,1)}) %reduce-scatter.2.cloned.1.call-update) | async-done | bytes 409616 | tf_op jit(solution)/shard_map/reduce_scatter | solution.py:149
  128.8 1.1 bitcast_add_fusion
  131.3 0.9 convolution_add_fusion.9
  139.1 0.9 maximum_maximum_fusion.1
  140.5 1.6 copy.25
  142.2 63.1 %all-gather.4.cloned.1.call-done = bf16[2560,2560]{1,0:T(8,128)(2,1)} async-done(((bf16[80,2560]{1,0:T(8,128)(2,1)}), bf16[2560,2560]{1,0:T(8,128)(2,1)}) %all-gather.4.cloned.1.call-update) | async-done | bytes 13107216 | tf_op jit(solution)/shard_map/all_gather | solution.py:168
  205.3 8.6 %shard_map.128 = (bf16[30,64,2560]{2,1,0:T(8,128)(2,1)}, bf16[16,2560]{1,0:T(8,128)(2,1)}) custom-call(s32[31]{0:T(128)} %clamp_bitcast_fusion.index_ref, bf16[32,80,2560]{2,1,0:T(8,128)(2,1)} %bitcast.93), custom_call_target="tpu_custom_call" | custom-call | bytes 19824640 | tf_op jit(solution)/shard_map/pallas_call | solution.py:61
  (69 shorter events, 17.8 us)
Async XLA Ops:
  7.2 4.8 %copy-start.5 = (bf16[128,1280]{1,0:T(8,128)(2,1)S(1)}, bf16[128,1280]{1,0:T(8,128)(2,1)}, u32[]{:S(2)}) copy-start(bf16[128,1280]{1,0:T(8,128)(2,1)} %param.12) | copy-start | bytes 983044
  7.2 121.6 %reduce-scatter.2.cloned.1.call-start = ((), (), s32[]{:S(2)}) async-start(), calls=%async_computation.4 | async-start | bytes 13516800 | tf_op jit(solution)/shard_map/reduce_scatter | solution.py:149
  13.4 1.1 copy-start
  13.4 1.3 copy-start.4
  21.4 0.8 copy-start.6
  21.4 183.9 %all-gather.4.cloned.1.call-start = ((), (), s32[]{:S(2)}) async-start(), calls=%async_computation.5 | async-start | bytes 13516800 | tf_op jit(solution)/shard_map/all_gather | solution.py:168
  68.0 21.7 %copy-start.1 = (f32[2,128,2560]{2,1,0:T(8,128)S(1)}, f32[2,128,2560]{2,1,0:T(8,128)}, u32[]{:S(2)}) copy-start(f32[2,128,2560]{2,1,0:T(8,128)} %param.17) | copy-start | bytes 7864324
  90.5 1.7 copy-start.2
  105.3 23.6 %copy-start.3 = (f32[1,74,2560]{2,0,1:T(1,128)S(1)}, f32[1,74,2560]{2,0,1:T(1,128)}, u32[]{:S(2)}) copy-start(f32[1,74,2560]{2,0,1:T(1,128)} %param.16) | copy-start | bytes 2273284
  139.0 1.0 copy-start.7
Sparse Core Ops, SparseCore 0:
  21.5 107.2 reduce-scatter.1
  140.1 65.1 all-gather.3

commit v12 on v9

--- a/solution.py
+++ b/solution.py
@@ -98,9 +98,8 @@
     f32, bf16 = jnp.float32, jnp.bfloat16
 
     owners = owner_deal[0]
-    head_owner = owners[:n_blocks]
-    dt_owner = owners[n_blocks]
     slots = jnp.arange(n_data, dtype=jnp.int32)
+    owner_hot = (owners[None, :] == slots[:, None]).astype(jnp.bfloat16)
 
     bc_cols = jnp.sum(lax.all_gather(bc_grad, "tensor", axis=0).astype(f32), axis=0)
     bc_total = bc_cols.shape[1]
@@ -132,12 +131,12 @@
     upper = jnp.concatenate([zx, jnp.zeros_like(io)], axis=2).reshape(tokens, n_blocks, HD)
     lower = jnp.concatenate([jnp.zeros_like(zx), io], axis=2).reshape(tokens, n_blocks, HD)
     grad_blocks = jnp.concatenate([upper, lower], axis=0)
-    pick = (head_owner[None, :] == slots[:, None]).astype(bf16)
+    pick = owner_hot[:, :n_blocks]
     owner_cols = jnp.einsum(
         "tbr,ob->tor", grad_blocks, pick, preferred_element_type=f32
     ).astype(bf16)
     dt_cols = jnp.concatenate([dt_grad, jnp.zeros_like(dt_grad)], axis=0)
-    is_dt = (slots == dt_owner).astype(bf16)
+    is_dt = owner_hot[:, n_blocks]
     dt_owner_cols = dt_cols[:, None, :] * is_dt[None, :, None]
     chunk = -(-capacity // 16) * 16
     pad_cols = jnp.zeros((2 * tokens, n_data, chunk - capacity), bf16)

time: 221 us -> 219 us (level)
  no operation moved by 1% of the time
where the time goes in v12:
time: 219 us
  blocking collectives  82.9 us (38%)
  waiting for transfers between devices  66.8 us (31%)
  matrix products  33.4 us (15%)
  between operations  14.5 us (7%)
  Pallas kernels  8.59 us (4%)
  local copies, waits for them, and re-layouts  7.71 us (4%)
  other arithmetic  5.07 us (2%)
    all_gather x1, waiting for transfers between devices, on_device(): everything = lax.all_gather(owned_update, 'dp', axis=0, tiled=False)  63.1 us
    all_to_all x1, blocking collectives, on_device(): lax.all_to_all(plane_copies, 'tensor', split_axis=0, concat_axis=0, tiled...  35.2 us
    all_to_all x1, blocking collectives, on_device(): lax.all_to_all(bc_part, 'dp', split_axis=0, concat_axis=0, tiled=True)  19 us
    all_to_all x1, blocking collectives, on_device(): lax.all_to_all(bc_copies, 'dp', split_axis=0, concat_axis=0, tiled=True)  16.3 us
    dot_general x10, matrix products, orthogonalize(): jnp.einsum('bij,bjk->bik', polynomial, current, precision=highest)  12.9 us
    all_gather x1, blocking collectives, on_device(): lax.all_gather(bc_grad, 'tensor', axis=0).astype(f32)  12.3 us
    dot_general x10, matrix products, orthogonalize(): jnp.einsum('bik,bjk->bij', current, current, precision=highest)  11 us
    pallas_call x1, Pallas kernels, gather_slabs(): pl.pallas_call(_gather_kernel, grid_spec=pltpu.PrefetchScalarGridSpec(num...  8.59 us
  transfers between devices with their start and end apart: 2, of which 2 were waited for; matrix products, arithmetic and copies ran while one was open for 10% of the time, Pallas kernels for 0%

profile of v12, /device:TPU:1, one launch (start us, length us, event | category | flops | bytes accessed | tf_op | source)
XLA Modules:
  0.0 219.0 jit_solution(1817376444258970197)
XLA Ops:
  8.1 1.1 copy.20
  13.0 6.6 %convolution_convert_fusion = bf16[2560,2560]{1,0:T(8,128)(2,1)} fusion(bf16[256,2560]{0,1:T(8,128)(2,1)S(1)} %bitcast.92, bf16[128,2560]{1,0:T(8,128)(2,1)S(1)} %copy-done.4, bf16[128,2560]{1,0:T(8,128)(2,1)S(1)} %copy-done), kind=kOutput, calls=%fused_computation | convolution fusion | flops 3364618240 | bytes 15728640 | tf_op jit(solution)/shard_map/dot_general | solution.py:147
  20.5 12.3 %all-gather = bf16[512,256]{1,0:T(8,128)(2,1)S(1)} all-gather(bf16[128,256]{1,0:T(8,128)(2,1)S(1)} %copy-done.6), channel_id=2, replica_groups=mesh['dp'=32,'tensor'=4] {'tensor'}, dimensions={0}, use_global_device_ids=true | all-gather | bytes 327680 | tf_op jit(solution)/shard_map/all_gather | solution.py:104
  33.5 19.0 %all_to_all.19 = bf16[32,2,2560]{2,1,0:T(2,128)(2,1)S(1)} all-to-all(bf16[32,2,2560]{2,1,0:T(2,128)(2,1)S(1)} %all_to_all.12), channel_id=1, replica_groups=mesh['dp'=32,'tensor'=4] {'dp'}, dimensions={0} | all-to-all | bytes 655360 | tf_op jit(solution)/shard_map/all_to_all | solution.py:118
  53.0 16.3 %all_to_all.20 = f32[32,2,2560]{2,1,0:T(2,128)S(1)} all-to-all(f32[32,2,2560]{2,1,0:T(2,128)S(1)} %broadcast_in_dim.13), channel_id=1, replica_groups=mesh['dp'=32,'tensor'=4] {'dp'}, dimensions={0} | all-to-all | bytes 1310720 | tf_op jit(solution)/shard_map/all_to_all | solution.py:121
  70.1 35.2 %all_to_all.21 = f32[4,64,2560]{2,1,0:T(8,128)S(1)} all-to-all(f32[4,64,2560]{2,1,0:T(8,128)S(1)} %broadcast_in_dim.15), channel_id=1, replica_groups=mesh['dp'=32,'tensor'=4] {'tensor'}, dimensions={0} | all-to-all | bytes 5242880 | tf_op jit(solution)/shard_map/all_to_all | solution.py:124
  106.0 1.4 fusion.21
  107.7 1.6 convolution_add_fusion.4
  109.3 1.4 fusion.33
  110.9 1.5 convolution_add_fusion.3
  112.5 1.4 fusion.34
  114.1 1.5 convolution_add_fusion.2
  115.7 1.4 fusion.35
  117.3 1.5 convolution_add_fusion.1
  118.9 1.6 fusion.36
  120.7 2.7 %fusion.1 = bf16[2,128,2560]{2,1,0:T(8,128)(2,1)} fusion(f32[2,128,128]{2,1,0:T(8,128)S(1)} %fusion.6, f32[2,128,2560]{2,1,0:T(8,128)S(1)} %convolution_add_fusion.1), kind=kOutput, calls=%fused_computation.7 | convolution fusion | flops 505937920 | bytes 4063232 | tf_op jit(solution)/shard_map/bij,bjk->bik/dot_general | solution.py:29
  123.4 3.7 %reduce-scatter.2.cloned.1.call-done = bf16[80,2560]{1,0:T(8,128)(2,1)} async-done(((bf16[2560,2560]{1,0:T(8,128)(2,1)}), bf16[80,2560]{1,0:T(8,128)(2,1)}) %reduce-scatter.2.cloned.1.call-update) | async-done | bytes 409616 | tf_op jit(solution)/shard_map/reduce_scatter | solution.py:148
  127.1 1.1 bitcast_add_fusion.1
  128.6 0.8 fusion.30
  129.6 0.9 convolution_add_fusion.9
  137.3 0.9 maximum_maximum_fusion.1
  138.8 1.6 copy.25
  140.5 63.1 %all-gather.4.cloned.1.call-done = bf16[2560,2560]{1,0:T(8,128)(2,1)} async-done(((bf16[80,2560]{1,0:T(8,128)(2,1)}), bf16[2560,2560]{1,0:T(8,128)(2,1)}) %all-gather.4.cloned.1.call-update) | async-done | bytes 13107216 | tf_op jit(solution)/shard_map/all_gather | solution.py:167
  203.5 8.6 %shard_map.128 = (bf16[30,64,2560]{2,1,0:T(8,128)(2,1)}, bf16[16,2560]{1,0:T(8,128)(2,1)}) custom-call(s32[31]{0:T(128)} %broadcast_clamp_fusion.index_ref, bf16[32,80,2560]{2,1,0:T(8,128)(2,1)} %bitcast.89), custom_call_target="tpu_custom_call" | custom-call | bytes 19824640 | tf_op jit(solution)/shard_map/pallas_call | solution.py:61
  (68 shorter events, 17.0 us)
Async XLA Ops:
  7.2 3.1 %copy-start.5 = (bf16[128,1280]{1,0:T(8,128)(2,1)S(1)}, bf16[128,1280]{1,0:T(8,128)(2,1)}, u32[]{:S(2)}) copy-start(bf16[128,1280]{1,0:T(8,128)(2,1)} %param.12) | copy-start | bytes 983044
  7.2 119.9 %reduce-scatter.2.cloned.1.call-start = ((), (), s32[]{:S(2)}) async-start(), calls=%async_computation.4 | async-start | bytes 13516800 | tf_op jit(solution)/shard_map/reduce_scatter | solution.py:148
  11.7 1.1 copy-start
  11.7 1.3 copy-start.4
  19.6 0.8 copy-start.6
  19.7 183.9 %all-gather.4.cloned.1.call-start = ((), (), s32[]{:S(2)}) async-start(), calls=%async_computation.5 | async-start | bytes 13516800 | tf_op jit(solution)/shard_map/all_gather | solution.py:167
  70.1 35.2 %copy-start.1 = (f32[2,128,2560]{2,1,0:T(8,128)S(1)}, f32[2,128,2560]{2,1,0:T(8,128)}, u32[]{:S(2)}) copy-start(f32[2,128,2560]{2,1,0:T(8,128)} %param.17) | copy-start | bytes 7864324
  106.0 1.7 copy-start.2
  120.7 6.4 %copy-start.3 = (f32[1,74,2560]{2,0,1:T(1,128)S(1)}, f32[1,74,2560]{2,0,1:T(1,128)}, u32[]{:S(2)}) copy-start(f32[1,74,2560]{2,0,1:T(1,128)} %param.16) | copy-start | bytes 2273284
  137.2 1.0 copy-start.7
Sparse Core Ops, SparseCore 0:
  19.8 107.2 reduce-scatter.1
  138.4 65.1 all-gather.3

commit v13 on v12

--- a/solution.py
+++ b/solution.py
@@ -126,15 +126,17 @@
     scale = math.sqrt(width)
     bc_update = (orthogonalize(bc_moment) * scale).astype(bf16)
 
-    zx = zx_grad.reshape(tokens, heads_here, 2, HD)
-    io = inner_out.reshape(tokens, heads_here, 1, HD)
-    upper = jnp.concatenate([zx, jnp.zeros_like(io)], axis=2).reshape(tokens, n_blocks, HD)
-    lower = jnp.concatenate([jnp.zeros_like(zx), io], axis=2).reshape(tokens, n_blocks, HD)
-    grad_blocks = jnp.concatenate([upper, lower], axis=0)
-    pick = owner_hot[:, :n_blocks]
-    owner_cols = jnp.einsum(
-        "tbr,ob->tor", grad_blocks, pick, preferred_element_type=f32
-    ).astype(bf16)
+    by_kind = owner_hot[:, :n_blocks].reshape(n_data, heads_here, 3)
+    zx_blocks = zx_grad.reshape(tokens, 2 * heads_here, HD)
+    io_blocks = inner_out.reshape(tokens, heads_here, HD)
+    owner_zx = jnp.einsum(
+        "tbr,ob->tor", zx_blocks, by_kind[:, :, :2].reshape(n_data, 2 * heads_here),
+        preferred_element_type=f32,
+    )
+    owner_io = jnp.einsum(
+        "tbr,ob->tor", io_blocks, by_kind[:, :, 2], preferred_element_type=f32
+    )
+    owner_cols = jnp.concatenate([owner_zx, owner_io], axis=0).astype(bf16)
     dt_cols = jnp.concatenate([dt_grad, jnp.zeros_like(dt_grad)], axis=0)
     is_dt = owner_hot[:, n_blocks]
     dt_owner_cols = dt_cols[:, None, :] * is_dt[None, :, None]

time: 219 us -> 220 us (level)
    unnamed x19 -> x17, local copies, waits for them, and re-layouts: 4.26 us -> 5.23 us
where the time goes in v13:
time: 220 us
  blocking collectives  82.9 us (38%)
  waiting for transfers between devices  66.8 us (30%)
  matrix products  33.8 us (15%)
  between operations  14.5 us (7%)
  Pallas kernels  8.59 us (4%)
  local copies, waits for them, and re-layouts  7.94 us (4%)
  other arithmetic  4.99 us (2%)
    all_gather x1, waiting for transfers between devices, on_device(): everything = lax.all_gather(owned_update, 'dp', axis=0, tiled=False)  63.2 us
    all_to_all x1, blocking collectives, on_device(): lax.all_to_all(plane_copies, 'tensor', split_axis=0, concat_axis=0, tiled...  35.2 us
    all_to_all x1, blocking collectives, on_device(): lax.all_to_all(bc_part, 'dp', split_axis=0, concat_axis=0, tiled=True)  19 us
    all_to_all x1, blocking collectives, on_device(): lax.all_to_all(bc_copies, 'dp', split_axis=0, concat_axis=0, tiled=True)  16.3 us
    dot_general x10, matrix products, orthogonalize(): jnp.einsum('bij,bjk->bik', polynomial, current, precision=highest)  12.9 us
    all_gather x1, blocking collectives, on_device(): lax.all_gather(bc_grad, 'tensor', axis=0).astype(f32)  12.3 us
    dot_general x10, matrix products, orthogonalize(): jnp.einsum('bik,bjk->bij', current, current, precision=highest)  11 us
    pallas_call x1, Pallas kernels, gather_slabs(): pl.pallas_call(_gather_kernel, grid_spec=pltpu.PrefetchScalarGridSpec(num...  8.59 us
  transfers between devices with their start and end apart: 2, of which 2 were waited for; matrix products, arithmetic and copies ran while one was open for 10% of the time, Pallas kernels for 0%

profile of v13, /device:TPU:1, one launch (start us, length us, event | category | flops | bytes accessed | tf_op | source)
XLA Modules:
  0.0 219.6 jit_solution(13669950455446498187)
XLA Ops:
  8.0 1.1 copy.23
  9.1 1.2 copy.20
  13.5 6.7 %convolution_convert_fusion = bf16[2560,2560]{1,0:T(8,128)(2,1)} fusion(bf16[256,2560]{0,1:T(8,128)(2,1)S(1)} %bitcast.97, bf16[128,2560]{1,0:T(8,128)(2,1)S(1)} %copy-done.4, bf16[128,2560]{1,0:T(8,128)(2,1)S(1)} %copy-done), kind=kOutput, calls=%fused_computation | convolution fusion | flops 3364618240 | bytes 15728640 | tf_op jit(solution)/shard_map/dot_general | solution.py:149
  21.0 12.3 %all-gather = bf16[512,256]{1,0:T(8,128)(2,1)S(1)} all-gather(bf16[128,256]{1,0:T(8,128)(2,1)S(1)} %copy-done.5), channel_id=2, replica_groups=mesh['dp'=32,'tensor'=4] {'tensor'}, dimensions={0}, use_global_device_ids=true | all-gather | bytes 327680 | tf_op jit(solution)/shard_map/all_gather | solution.py:104
  34.0 19.0 %all_to_all.19 = bf16[32,2,2560]{2,1,0:T(2,128)(2,1)S(1)} all-to-all(bf16[32,2,2560]{2,1,0:T(2,128)(2,1)S(1)} %all_to_all.12), channel_id=1, replica_groups=mesh['dp'=32,'tensor'=4] {'dp'}, dimensions={0} | all-to-all | bytes 655360 | tf_op jit(solution)/shard_map/all_to_all | solution.py:118
  53.5 16.3 %all_to_all.20 = f32[32,2,2560]{2,1,0:T(2,128)S(1)} all-to-all(f32[32,2,2560]{2,1,0:T(2,128)S(1)} %broadcast_in_dim.13), channel_id=1, replica_groups=mesh['dp'=32,'tensor'=4] {'dp'}, dimensions={0} | all-to-all | bytes 1310720 | tf_op jit(solution)/shard_map/all_to_all | solution.py:121
  70.6 35.2 %all_to_all.21 = f32[4,64,2560]{2,1,0:T(8,128)S(1)} all-to-all(f32[4,64,2560]{2,1,0:T(8,128)S(1)} %broadcast_in_dim.15), channel_id=1, replica_groups=mesh['dp'=32,'tensor'=4] {'tensor'}, dimensions={0} | all-to-all | bytes 5242880 | tf_op jit(solution)/shard_map/all_to_all | solution.py:124
  106.6 1.4 fusion.19
  108.2 1.6 convolution_add_fusion.4
  109.8 1.4 fusion.33
  111.5 1.5 convolution_add_fusion.3
  113.0 1.4 fusion.34
  114.6 1.5 convolution_add_fusion.2
  116.2 1.4 fusion.35
  117.8 1.5 convolution_add_fusion.1
  119.4 1.6 fusion.36
  121.3 2.7 %fusion.1 = bf16[2,128,2560]{2,1,0:T(8,128)(2,1)} fusion(f32[2,128,128]{2,1,0:T(8,128)S(1)} %fusion.7, f32[2,128,2560]{2,1,0:T(8,128)S(1)} %convolution_add_fusion.1), kind=kOutput, calls=%fused_computation.7 | convolution fusion | flops 505937920 | bytes 4063232 | tf_op jit(solution)/shard_map/bij,bjk->bik/dot_general | solution.py:29
  124.0 3.6 %reduce-scatter.2.cloned.1.call-done = bf16[80,2560]{1,0:T(8,128)(2,1)} async-done(((bf16[2560,2560]{1,0:T(8,128)(2,1)}), bf16[80,2560]{1,0:T(8,128)(2,1)}) %reduce-scatter.2.cloned.1.call-update) | async-done | bytes 409616 | tf_op jit(solution)/shard_map/reduce_scatter | solution.py:150
  127.6 1.1 bitcast_add_fusion.1
  130.1 0.9 convolution_add_fusion.9
  137.8 0.9 maximum_maximum_fusion.1
  139.3 1.6 copy.26
  140.9 63.2 %all-gather.4.cloned.1.call-done = bf16[2560,2560]{1,0:T(8,128)(2,1)} async-done(((bf16[80,2560]{1,0:T(8,128)(2,1)}), bf16[2560,2560]{1,0:T(8,128)(2,1)}) %all-gather.4.cloned.1.call-update) | async-done | bytes 13107216 | tf_op jit(solution)/shard_map/all_gather | solution.py:169
  204.1 8.6 %shard_map.128 = (bf16[30,64,2560]{2,1,0:T(8,128)(2,1)}, bf16[16,2560]{1,0:T(8,128)(2,1)}) custom-call(s32[31]{0:T(128)} %broadcast_clamp_fusion.index_ref, bf16[32,80,2560]{2,1,0:T(8,128)(2,1)} %bitcast.94), custom_call_target="tpu_custom_call" | custom-call | bytes 19824640 | tf_op jit(solution)/shard_map/pallas_call | solution.py:61
  (66 shorter events, 17.1 us)
Async XLA Ops:
  7.2 120.4 %reduce-scatter.2.cloned.1.call-start = ((), (), s32[]{:S(2)}) async-start(), calls=%async_computation.4 | async-start | bytes 13516800 | tf_op jit(solution)/shard_map/reduce_scatter | solution.py:150
  12.2 1.1 copy-start
  12.2 1.3 copy-start.4
  20.2 0.8 copy-start.5
  20.2 183.9 %all-gather.4.cloned.1.call-start = ((), (), s32[]{:S(2)}) async-start(), calls=%async_computation.5 | async-start | bytes 13516800 | tf_op jit(solution)/shard_map/all_gather | solution.py:169
  70.6 35.2 %copy-start.1 = (f32[2,128,2560]{2,1,0:T(8,128)S(1)}, f32[2,128,2560]{2,1,0:T(8,128)}, u32[]{:S(2)}) copy-start(f32[2,128,2560]{2,1,0:T(8,128)} %param.17) | copy-start | bytes 7864324
  106.5 1.7 copy-start.2
  121.3 6.3 %copy-start.3 = (f32[1,74,2560]{2,0,1:T(1,128)S(1)}, f32[1,74,2560]{2,0,1:T(1,128)}, u32[]{:S(2)}) copy-start(f32[1,74,2560]{2,0,1:T(1,128)} %param.16) | copy-start | bytes 2273284
  137.7 1.0 copy-start.6
Sparse Core Ops, SparseCore 0:
  20.3 107.2 reduce-scatter.1
  138.9 65.2 all-gather.3

commit v14 on v12

--- a/solution.py
+++ b/solution.py
@@ -131,18 +131,18 @@
     upper = jnp.concatenate([zx, jnp.zeros_like(io)], axis=2).reshape(tokens, n_blocks, HD)
     lower = jnp.concatenate([jnp.zeros_like(zx), io], axis=2).reshape(tokens, n_blocks, HD)
     grad_blocks = jnp.concatenate([upper, lower], axis=0)
-    pick = owner_hot[:, :n_blocks]
-    owner_cols = jnp.einsum(
-        "tbr,ob->tor", grad_blocks, pick, preferred_element_type=f32
-    ).astype(bf16)
+    chunk = -(-capacity // 16) * 16
     dt_cols = jnp.concatenate([dt_grad, jnp.zeros_like(dt_grad)], axis=0)
-    is_dt = owner_hot[:, n_blocks]
-    dt_owner_cols = dt_cols[:, None, :] * is_dt[None, :, None]
-    chunk = -(-capacity // 16) * 16
-    pad_cols = jnp.zeros((2 * tokens, n_data, chunk - capacity), bf16)
-    send_cols = jnp.concatenate([owner_cols, dt_owner_cols, pad_cols], axis=2).reshape(
-        2 * tokens, n_data * chunk
+    all_blocks = jnp.concatenate(
+        [
+            jnp.pad(grad_blocks, ((0, 0), (0, 0), (0, chunk - HD))),
+            jnp.pad(dt_cols, ((0, 0), (HD, chunk - capacity)))[:, None, :],
+        ],
+        axis=1,
     )
+    send_cols = jnp.einsum(
+        "tbr,ob->tor", all_blocks, owner_hot, preferred_element_type=f32
+    ).astype(bf16).reshape(2 * tokens, n_data * chunk)
     factors = jnp.concatenate([layer_input, out_grad], axis=0)
     send = lax.dot_general(send_cols, factors, contract, preferred_element_type=f32).astype(bf16)
     owned = lax.psum_scatter(send, "dp", scatter_dimension=0, tiled=True)

time: 219 us -> 219 us (level)
  blocking collectives: 82.9 us -> 47.7 us
  waiting for transfers between devices: 66.8 us -> 94.6 us
  starting transfers between devices: 0.08 us -> 4.18 us
    all_to_all x1 -> x0, blocking collectives: 35.2 us -> none  [on_device(): lax.all_to_all(plane_copies, 'tensor', split_axis=0, concat_axis=0, tiled...]
    all_to_all x0 -> x1, waiting for transfers between devices: none -> 31.2 us  [on_device(): lax.all_to_all(plane_copies, 'tensor', split_axis=0, concat_axis=0, tiled...]
    all_to_all x0 -> x1, starting transfers between devices: none -> 4.14 us  [on_device(): lax.all_to_all(plane_copies, 'tensor', split_axis=0, concat_axis=0, tiled...]
    reduce_scatter x1, waiting for transfers between devices: 3.66 us -> 0.16 us  [on_device(): owned = lax.psum_scatter(send, 'dp', scatter_dimension=0, tiled=True)]
    unnamed x19 -> x17, local copies, waits for them, and re-layouts: 4.26 us -> 4.74 us
  transfers between devices with their start and end apart: 2 -> 3, of which waited for: 2 -> 3; matrix products, arithmetic and copies ran while one was open for 10% -> 12% of each run, Pallas kernels for 0% -> 0%
where the time goes in v14:
time: 219 us
  waiting for transfers between devices  94.6 us (43%)
  blocking collectives  47.7 us (22%)
  matrix products  33.5 us (15%)
  between operations  14.5 us (7%)
  local copies, waits for them, and re-layouts  9.79 us (4%)
  Pallas kernels  8.59 us (4%)
  other arithmetic  5.77 us (3%)
  starting transfers between devices  4.18 us (2%)
    all_gather x1, waiting for transfers between devices, on_device(): everything = lax.all_gather(owned_update, 'dp', axis=0, tiled=False)  63.2 us
    all_to_all x1, waiting for transfers between devices, on_device(): lax.all_to_all(plane_copies, 'tensor', split_axis=0, concat_axis=0, tiled...  31.2 us
    all_to_all x1, blocking collectives, on_device(): lax.all_to_all(bc_part, 'dp', split_axis=0, concat_axis=0, tiled=True)  19 us
    all_to_all x1, blocking collectives, on_device(): lax.all_to_all(bc_copies, 'dp', split_axis=0, concat_axis=0, tiled=True)  16.3 us
    dot_general x10, matrix products, orthogonalize(): jnp.einsum('bij,bjk->bik', polynomial, current, precision=highest)  12.9 us
    all_gather x1, blocking collectives, on_device(): lax.all_gather(bc_grad, 'tensor', axis=0).astype(f32)  12.3 us
    dot_general x10, matrix products, orthogonalize(): jnp.einsum('bik,bjk->bij', current, current, precision=highest)  11.1 us
    pallas_call x1, Pallas kernels, gather_slabs(): pl.pallas_call(_gather_kernel, grid_spec=pltpu.PrefetchScalarGridSpec(num...  8.59 us
  transfers between devices with their start and end apart: 3, of which 3 were waited for; matrix products, arithmetic and copies ran while one was open for 12% of the time, Pallas kernels for 0%

profile of v14, /device:TPU:1, one launch (start us, length us, event | category | flops | bytes accessed | tf_op | source)
XLA Modules:
  0.0 218.6 jit_solution(9756689136320752203)
XLA Ops:
  8.0 1.1 copy.20
  12.6 6.7 %convolution_convert_fusion = bf16[2560,2560]{1,0:T(8,128)(2,1)} fusion(bf16[256,2560]{0,1:T(8,128)(2,1)S(1)} %bitcast.94, bf16[128,2560]{1,0:T(8,128)(2,1)S(1)} %copy-done.3, bf16[128,2560]{1,0:T(8,128)(2,1)S(1)} %copy-done), kind=kOutput, calls=%fused_computation | convolution fusion | flops 3364618240 | bytes 15728640 | tf_op jit(solution)/shard_map/dot_general | solution.py:147
  20.1 12.3 %all-gather = bf16[512,256]{1,0:T(8,128)(2,1)S(1)} all-gather(bf16[128,256]{1,0:T(8,128)(2,1)S(1)} %copy-done.5), channel_id=2, replica_groups=mesh['dp'=32,'tensor'=4] {'tensor'}, dimensions={0}, use_global_device_ids=true | all-gather | bytes 327680 | tf_op jit(solution)/shard_map/all_gather | solution.py:104
  33.1 19.0 %all_to_all.19 = bf16[32,2,2560]{2,1,0:T(2,128)(2,1)S(1)} all-to-all(bf16[32,2,2560]{2,1,0:T(2,128)(2,1)S(1)} %all_to_all.12), channel_id=1, replica_groups=mesh['dp'=32,'tensor'=4] {'dp'}, dimensions={0} | all-to-all | bytes 655360 | tf_op jit(solution)/shard_map/all_to_all | solution.py:118
  52.6 16.3 %all_to_all.20 = f32[32,2,2560]{2,1,0:T(2,128)S(1)} all-to-all(f32[32,2,2560]{2,1,0:T(2,128)S(1)} %broadcast_in_dim.13), channel_id=1, replica_groups=mesh['dp'=32,'tensor'=4] {'dp'}, dimensions={0} | all-to-all | bytes 1310720 | tf_op jit(solution)/shard_map/all_to_all | solution.py:121
  69.4 1.8 broadcast_in_dim.15
  71.2 4.1 %all-to-all-start.2 = ((f32[4,64,2560]{2,1,0:T(8,128)}), f32[4,64,2560]{2,1,0:T(8,128)S(1)}, u32[]{:S(2)}, u32[]{:S(2)}) async-start(f32[4,64,2560]{2,1,0:T(8,128)} %broadcast_in_dim.15), calls=%async_computation.3 | async-start | bytes 5242880 | tf_op jit(solution)/shard_map/all_to_all | solution.py:124
  75.4 31.2 %all-to-all-done.2 = f32[4,64,2560]{2,1,0:T(8,128)S(1)} async-done(((f32[4,64,2560]{2,1,0:T(8,128)}), f32[4,64,2560]{2,1,0:T(8,128)S(1)}, u32[]{:S(2)}, u32[]{:S(2)}) %all-to-all-start.2) | async-done | bytes 2621472 | tf_op jit(solution)/shard_map/all_to_all | solution.py:124
  106.6 2.3 %multiply_reduce_fusion = (f32[2]{0:T(128)S(1)}, f32[2,128,2560]{2,1,0:T(8,128)S(1)}) fusion(f32[2,128,2560]{2,1,0:T(8,128)} %param.17, f32[2,128,2560]{2,1,0:T(8,128)S(1)} %bitcast.92), kind=kLoop, calls=%fused_computation.18 | loop fusion | flops 2621438 | bytes 7864328 | tf_op jit(solution)/shard_map/reduce_sum | solution.py:22
  108.9 1.4 fusion.24
  110.6 1.6 convolution_add_fusion.4
  112.2 1.4 fusion.38
  113.8 1.5 convolution_add_fusion.3
  115.4 1.4 fusion.39
  117.0 1.5 convolution_add_fusion.2
  118.6 1.4 fusion.40
  120.2 1.5 convolution_add_fusion.1
  121.8 1.7 fusion.41
  123.7 2.7 %fusion.1 = bf16[2,128,2560]{2,1,0:T(8,128)(2,1)} fusion(f32[2,128,128]{2,1,0:T(8,128)S(1)} %fusion.12, f32[2,128,2560]{2,1,0:T(8,128)S(1)} %convolution_add_fusion.1), kind=kOutput, calls=%fused_computation.7 | convolution fusion | flops 505937920 | bytes 4063232 | tf_op jit(solution)/shard_map/bij,bjk->bik/dot_general | solution.py:29
  126.5 1.1 bitcast_add_fusion.1
  129.0 0.9 convolution_add_fusion.9
  138.3 1.6 copy.26
  139.9 63.2 %all-gather.4.cloned.1.call-done = bf16[2560,2560]{1,0:T(8,128)(2,1)} async-done(((bf16[80,2560]{1,0:T(8,128)(2,1)}), bf16[2560,2560]{1,0:T(8,128)(2,1)}) %all-gather.4.cloned.1.call-update) | async-done | bytes 13107216 | tf_op jit(solution)/shard_map/all_gather | solution.py:167
  203.2 8.6 %shard_map.128 = (bf16[30,64,2560]{2,1,0:T(8,128)(2,1)}, bf16[16,2560]{1,0:T(8,128)(2,1)}) custom-call(s32[31]{0:T(128)} %broadcast_clamp_fusion.index_ref, bf16[32,80,2560]{2,1,0:T(8,128)(2,1)} %bitcast.91), custom_call_target="tpu_custom_call" | custom-call | bytes 19824640 | tf_op jit(solution)/shard_map/pallas_call | solution.py:61
  (65 shorter events, 17.5 us)
Async XLA Ops:
  7.2 2.4 %copy-start.4 = (bf16[128,1280]{1,0:T(8,128)(2,1)S(1)}, bf16[128,1280]{1,0:T(8,128)(2,1)}, u32[]{:S(2)}) copy-start(bf16[128,1280]{1,0:T(8,128)(2,1)} %param.12) | copy-start | bytes 983044
  7.2 119.4 %reduce-scatter.2.cloned.1.call-start = ((), (), s32[]{:S(2)}) async-start(), calls=%async_computation.4 | async-start | bytes 13516800 | tf_op jit(solution)/shard_map/reduce_scatter | solution.py:148
  10.1 0.7 copy-start.6
  11.3 1.1 copy-start
  11.3 1.3 copy-start.3
  19.2 0.8 copy-start.5
  71.2 35.4 %all-to-all-start.2 = ((f32[4,64,2560]{2,1,0:T(8,128)}), f32[4,64,2560]{2,1,0:T(8,128)S(1)}, u32[]{:S(2)}, u32[]{:S(2)}) async-start(f32[4,64,2560]{2,1,0:T(8,128)} %broadcast_in_dim.15), calls=%async_computation.3 | async-start | bytes 5242880 | tf_op jit(solution)/shard_map/all_to_all | solution.py:124
  75.3 127.8 %all-gather.4.cloned.1.call-start = ((), (), s32[]{:S(2)}) async-start(), calls=%async_computation.5 | async-start | bytes 13516800 | tf_op jit(solution)/shard_map/all_gather | solution.py:167
  108.9 1.7 copy-start.1
  123.7 2.9 %copy-start.2 = (f32[1,74,2560]{2,0,1:T(1,128)S(1)}, f32[1,74,2560]{2,0,1:T(1,128)}, u32[]{:S(2)}) copy-start(f32[1,74,2560]{2,0,1:T(1,128)} %param.16) | copy-start | bytes 2273284
Sparse Core Ops, SparseCore 0:
  19.4 107.1 reduce-scatter.1
  137.8 65.3 all-gather.3
